TPU v7x, 1024 devices: a whole 4x4x32 slice. The times are simulated.
1024 devices in a mesh: chan: 32 (over z_lo, x), slab: 32 (over y, z_hi, core).
Axes of the slice: x: 4, y: 4, z: 32 (z_hi: 4, z_lo: 8; z = z_hi * 8 + z_lo), core: 2. Of those that a mesh axis runs over, the one named last changes fastest.
Arguments:
- inputs: bfloat16 [256, 32, 8, 128], P('chan', 'slab'), may hold values from -6 to 6
- weight: bfloat16 [256, 3, 3, 3, 256], P('chan'), may hold values from -0.078125 to 0.078125
- conv_bias: bfloat16 [256], P('chan'), may hold values from -3 to 3
- out_grad: bfloat16 [256, 32, 8, 128], P('chan', 'slab'), may hold values from -6 to 6
Outputs:
- activated: bfloat16 [256, 32, 8, 128], P('chan', 'slab')
- input_grad: bfloat16 [256, 32, 8, 128], P('chan', 'slab')
- weight_grad: float32 [256, 3, 3, 3, 256], P('chan')
- bias_grad: float32 [256], P('chan')
All inputs are finite; a program needn't handle non-finite values.
Results may differ from a plain program's by a relative error of at most 0.006.
Values may be sent and summed in bfloat16 or wider, within the bound.
No kernel may reach another device: no remote copies, remote signals or barrier semaphores. Data moves between devices by JAX's collectives and lax.ppermute only.
A program may use at most 32 MiB of HBM per device.

v0:
```python
import math

import jax
import jax.numpy as jnp
from jax import lax
from jax.sharding import PartitionSpec as P


def padded(cells, sides, width):
    for axis, dim in sides:
        count = lax.axis_size(axis)
        ends = count - 1
        head = lax.slice_in_dim(cells, 0, width, axis=dim)
        tail = lax.slice_in_dim(cells, cells.shape[dim] - width, cells.shape[dim], axis=dim)
        cells = jnp.concatenate(
            [
                lax.ppermute(tail, axis, [(i, (i + 1) % count) for i in range(ends)]),
                cells,
                lax.ppermute(head, axis, [((i + 1) % count, i) for i in range(ends)]),
            ],
            axis=dim,
        )
    return cells


def copy_for_each(shard, axis):
    copies = jnp.broadcast_to(shard, (lax.axis_size(axis), *shard.shape))
    return lax.all_to_all(copies, axis, split_axis=0, concat_axis=0, tiled=True)


def joined_along(blocks, dim):
    shape = list(blocks.shape[1:])
    shape[dim] *= blocks.shape[0]
    return jnp.moveaxis(blocks, 0, dim).reshape(shape)


def gather_directly(shard, axis, dim):
    blocks = copy_for_each(shard, axis)
    return joined_along(blocks, dim)


def sent_together(arrays, axis, dim, along):
    columns = [a.reshape(*a.shape[:along], -1) for a in arrays]
    both = jnp.concatenate(columns, axis=along)
    whole, at, gathered = (lax.all_gather(both, axis, axis=dim, tiled=True), 0, [])
    for a, column in zip(arrays, columns):
        slab = whole[..., at : at + column.shape[along]]
        gathered.append(slab.reshape(*slab.shape[:along], *a.shape[along:]))
        at += column.shape[along]
    return tuple(gathered)


def silu_grad(values):
    sig = jax.nn.sigmoid(values)
    return sig * (1.0 + values * (1.0 - sig))


def shifted_cells(values, high_step, wide_step, n_high, n_wide):
    length = values.shape[-1]
    offset = high_step * n_wide + wide_step
    if offset > 0:
        filler = jnp.zeros(values.shape[:-1] + (offset,), values.dtype)
        moved = jnp.concatenate([values[..., offset:], filler], axis=-1)
    elif offset < 0:
        filler = jnp.zeros(values.shape[:-1] + (-offset,), values.dtype)
        moved = jnp.concatenate([filler, values[..., :offset]], axis=-1)
    else:
        moved = values
    position = lax.iota(jnp.int32, length)
    high_index = position // n_wide % n_high + high_step
    wide_index = position % n_wide + wide_step
    valid = (high_index >= 0) & (high_index < n_high) & (wide_index >= 0) & (wide_index < n_wide)
    return jnp.where(valid, moved, jnp.zeros_like(moved))


def back_block(slope_flat, kernel_cols, n_local, cells, n_high, n_wide):
    in_rows = slope_flat.shape[0]
    plane = n_high * n_wide
    summed = jnp.zeros((n_local, cells), jnp.float32)
    for depth_tap in range(3):
        back_slab = slope_flat[:, (2 - depth_tap) * plane : (2 - depth_tap) * plane + cells]
        weight_taps = kernel_cols[:, depth_tap].reshape(in_rows, 9 * n_local)
        products = lax.dot_general(
            weight_taps, back_slab, (((0,), (0,)), ((), ())), preferred_element_type=jnp.float32
        )
        products = products.reshape(3, 3, n_local, cells)
        for high_tap in range(3):
            for wide_tap in range(3):
                summed = summed + shifted_cells(
                    products[high_tap, wide_tap], 1 - high_tap, 1 - wide_tap, n_high, n_wide
                )
    return summed


def on_device(inputs, weight, conv_bias, out_grad):
    n_local, n_depth, n_high, n_wide = inputs.shape
    n_chan = weight.shape[4]
    plane = n_high * n_wide
    cells = n_depth * plane
    grad_scale = 1.0 / math.sqrt(cells * lax.axis_size("slab"))
    rimmed = padded(inputs, (("slab", 1),), 1)
    gathered_all = gather_directly(rimmed, "chan", 0)
    gathered_flat = gathered_all.reshape(n_chan, (n_depth + 2) * plane)
    in_planes = [
        gathered_flat[:, depth_tap * plane : depth_tap * plane + cells] for depth_tap in range(3)
    ]
    pre_sum = jnp.zeros((n_local, cells), jnp.float32)
    for depth_tap in range(3):
        weight_taps = jnp.transpose(weight[:, depth_tap], (1, 2, 0, 3)).reshape(9 * n_local, n_chan)
        products = jnp.dot(weight_taps, in_planes[depth_tap], preferred_element_type=jnp.float32)
        products = products.reshape(3, 3, n_local, cells)
        for high_tap in range(3):
            for wide_tap in range(3):
                pre_sum = pre_sum + shifted_cells(
                    products[high_tap, wide_tap], high_tap - 1, wide_tap - 1, n_high, n_wide
                )
    pre_sum = pre_sum + conv_bias.astype(jnp.float32)[:, None]
    activated = jax.nn.silu(pre_sum).astype(jnp.bfloat16).reshape(inputs.shape)
    slope = (out_grad.reshape(n_local, cells).astype(jnp.float32) * silu_grad(pre_sum)).astype(
        jnp.bfloat16
    )
    slope_moved = jnp.stack(
        [
            shifted_cells(slope, 1 - high_tap, 1 - wide_tap, n_high, n_wide)
            for high_tap in range(3)
            for wide_tap in range(3)
        ],
        axis=0,
    ).reshape(9 * n_local, cells)
    kernel_list = []
    for depth_tap in range(3):
        tap_grad = lax.dot_general(
            slope_moved,
            in_planes[depth_tap],
            (((1,), (1,)), ((), ())),
            preferred_element_type=jnp.float32,
        )
        kernel_list.append(jnp.transpose(tap_grad.reshape(3, 3, n_local, n_chan), (2, 0, 1, 3)))
    kernel_part = jnp.stack(kernel_list, axis=1)
    bias_part = jnp.sum(slope.astype(jnp.float32), axis=1)
    kernel_total, bias_total = lax.psum((kernel_part, bias_part), "slab")
    slope_rim = padded(slope.reshape(n_local, n_depth, n_high, n_wide), (("slab", 1),), 1)
    own_start = lax.axis_index("chan") * n_local
    grad_piece, weight_piece = sent_together((slope_rim, weight), "chan", 0, 2)
    own_cols = lax.dynamic_slice_in_dim(weight_piece, own_start, n_local, 4)
    grad_flat = grad_piece.reshape(grad_piece.shape[0], -1)
    back_total = back_block(grad_flat, own_cols, n_local, cells, n_high, n_wide)
    input_grad = back_total.astype(jnp.bfloat16).reshape(inputs.shape)
    return (activated, input_grad, kernel_total * grad_scale, bias_total * grad_scale)


def solution(mesh):
    placed = (
        P("chan", "slab", None, None),
        P("chan", None, None, None, None),
        P("chan"),
        P("chan", "slab", None, None),
    )
    return jax.shard_map(
        on_device,
        mesh=mesh,
        in_specs=placed,
        out_specs=(
            P("chan", "slab", None, None),
            P("chan", "slab", None, None),
            P("chan", None, None, None, None),
            P("chan"),
        ),
        check_vma=False,
    )
```

profile of v0, /device:TPU:1, one launch (start us, length us, event | category | flops | bytes accessed | tf_op | source)
XLA Modules:
  0.0 653.6 jit_solution(12489138598741446321)
XLA Ops:
  8.0 16.8 %collective-permute-start = (bf16[8,1,8,128]{3,2,1,0:T(8,128)(2,1)}, bf16[8,1,8,128]{3,2,1,0:T(8,128)(2,1)S(1)}, u32[]{:S(2)}, u32[]{:S(2)}) collective-permute-start(bf16[8,1,8,128]{3,2,1,0:T(8,128)(2,1)} %param.4), channel_id=1, source_target_pairs={{0,1},{1,2},{2,3},{3,4},{4,5},{5,6},{6,7},{7,8},{8,9},{9,10},{10,1... | collective-permute-start | bytes 49160 | tf_op jit(solution)/shard_map/ppermute | solution.py:17
  24.8 1.9 collective-permute-start.1
  26.8 12.0 %collective-permute-done.1 = bf16[8,1,8,128]{3,2,1,0:T(8,128)(2,1)S(1)} collective-permute-done((bf16[8,1,8,128]{3,2,1,0:T(8,128)(2,1)}, bf16[8,1,8,128]{3,2,1,0:T(8,128)(2,1)S(1)}, u32[]{:S(2)}, u32[]{:S(2)}) %collective-permute-start.1) | collective-permute-done | bytes 16416 | tf_op jit(solution)/shard_map/ppermute | solution.py:19
  38.8 0.7 pad_maximum_fusion.2
  39.6 1.6 broadcast_in_dim.196
  41.1 15.2 %all-to-all-start = ((bf16[32,8,3,8,128]{4,1,3,2,0:T(8,128)(2,1)}), bf16[32,8,3,8,128]{4,1,3,2,0:T(8,128)(2,1)S(1)}, u32[]{:S(2)}, u32[]{:S(2)}) async-start(bf16[32,8,3,8,128]{4,1,3,2,0:T(8,128)(2,1)} %broadcast_in_dim.196), calls=%async_computation | async-start | bytes 3145728 | tf_op jit(solution)/shard_map/all_to_all | solution.py:28
  56.6 64.0 %all-to-all-done = bf16[32,8,3,8,128]{4,1,3,2,0:T(8,128)(2,1)S(1)} async-done(((bf16[32,8,3,8,128]{4,1,3,2,0:T(8,128)(2,1)}), bf16[32,8,3,8,128]{4,1,3,2,0:T(8,128)(2,1)S(1)}, u32[]{:S(2)}, u32[]{:S(2)}) %all-to-all-start) | async-done | bytes 1572896 | tf_op jit(solution)/shard_map/all_to_all | solution.py:28
  120.6 0.2 fusion.7
  120.8 0.2 fusion.10
  121.0 0.2 fusion.13
  122.1 0.3 convert_reduce_fusion
  122.4 1.9 collective-permute-start.3
  124.3 12.4 %collective-permute-start.2 = (bf16[8,1,8,128]{3,0,2,1:T(8,128)(2,1)S(1)}, bf16[8,1,8,128]{3,0,2,1:T(8,128)(2,1)S(1)}, u32[]{:S(2)}, u32[]{:S(2)}) collective-permute-start(bf16[8,1,8,128]{3,0,2,1:T(8,128)(2,1)S(1)} %bitcast.393), channel_id=1, source_target_pairs={{0,1},{1,2},{2,3},{3,4},{4,5},{5,6},{6,7},{7,8},{8,9},{9,10},{10,1... | collective-permute-start | bytes 49160 | tf_op jit(solution)/shard_map/ppermute | solution.py:17
  137.3 0.3 convolution_bitcast_fusion
  137.6 0.3 convolution_bitcast_fusion.1
  137.9 0.3 convolution_bitcast_fusion.2
  138.2 0.7 pad_maximum_fusion
  139.0 0.7 pad_maximum_fusion.1
  139.7 129.3 %psum.15 = f32[8]{0:T(128)S(1)} all-reduce(f32[8]{0:T(128)S(1)} %get-tuple-element.12), channel_id=1, replica_groups=mesh['chan'=32,'slab'=32] {'slab'}, use_global_device_ids=true, to_apply=%region_2.3 | all-reduce | flops 8 | bytes 64 | tf_op jit(solution)/shard_map/psum | solution.py:141
  269.1 0.6 copy.21
  269.7 0.5 broadcast_multiply_fusion.1
  270.2 361.7 %all-reduce.58.cloned.1.call-done = f32[8,3,3,3,256]{4,0,3,2,1:T(8,128)} async-done(((f32[8,3,3,3,256]{4,0,3,2,1:T(8,128)}), f32[8,3,3,3,256]{4,0,3,2,1:T(8,128)}) %all-reduce.58.cloned.1.call-update) | async-done | bytes 221200 | tf_op jit(solution)/shard_map/psum | solution.py:141
  631.9 1.6 broadcast_multiply_fusion
  633.6 2.0 slice-done
  635.6 3.6 copy.16
  639.2 1.4 slice-done.1
  640.6 0.7 copy.17
  641.3 1.1 fusion.2
  642.3 1.1 fusion.1
  643.7 1.1 fusion
  645.4 0.2 fusion.71
  645.5 0.6 copy.22
  (101 shorter events, 2.3 us)
Async XLA Ops:
  8.0 18.8 %collective-permute-start = (bf16[8,1,8,128]{3,2,1,0:T(8,128)(2,1)}, bf16[8,1,8,128]{3,2,1,0:T(8,128)(2,1)S(1)}, u32[]{:S(2)}, u32[]{:S(2)}) collective-permute-start(bf16[8,1,8,128]{3,2,1,0:T(8,128)(2,1)} %param.4), channel_id=1, source_target_pairs={{0,1},{1,2},{2,3},{3,4},{4,5},{5,6},{6,7},{7,8},{8,9},{9,10},{10,1... | collective-permute-start | bytes 49160 | tf_op jit(solution)/shard_map/ppermute | solution.py:17
  24.8 14.0 %collective-permute-start.1 = (bf16[8,1,8,128]{3,2,1,0:T(8,128)(2,1)}, bf16[8,1,8,128]{3,2,1,0:T(8,128)(2,1)S(1)}, u32[]{:S(2)}, u32[]{:S(2)}) collective-permute-start(bf16[8,1,8,128]{3,2,1,0:T(8,128)(2,1)} %param.4), channel_id=1, source_target_pairs={{1,0},{2,1},{3,2},{4,3},{5,4},{6,5},{7,6},{8,7},{9,8},{10,9},{11,1... | collective-permute-start | bytes 49160 | tf_op jit(solution)/shard_map/ppermute | solution.py:19
  41.1 15.3 %copy-start.12 = (bf16[8]{0:T(256)(128)(2,1)S(1)}, bf16[8]{0:T(256)(128)(2,1)}, u32[]{:S(2)}) copy-start(bf16[8]{0:T(256)(128)(2,1)} %param.6) | copy-start | bytes 52
  41.1 15.4 %copy-start.9 = (bf16[8,1,8,128]{3,2,1,0:T(8,128)(2,1)S(1)}, bf16[8,1,8,128]{3,2,1,0:T(8,128)(2,1)}, u32[]{:S(2)}) copy-start(bf16[8,1,8,128]{3,2,1,0:T(8,128)(2,1)} %param.7) | copy-start | bytes 49156
  41.1 15.5 %copy-start = (bf16[8,3,3,3,256]{4,0,3,2,1:T(8,128)(2,1)S(1)}, bf16[8,3,3,3,256]{4,0,3,2,1:T(8,128)(2,1)}, u32[]{:S(2)}) copy-start(bf16[8,3,3,3,256]{4,0,3,2,1:T(8,128)(2,1)} %param.5) | copy-start | bytes 331780
  41.1 79.5 %all-to-all-start = ((bf16[32,8,3,8,128]{4,1,3,2,0:T(8,128)(2,1)}), bf16[32,8,3,8,128]{4,1,3,2,0:T(8,128)(2,1)S(1)}, u32[]{:S(2)}, u32[]{:S(2)}) async-start(bf16[32,8,3,8,128]{4,1,3,2,0:T(8,128)(2,1)} %broadcast_in_dim.196), calls=%async_computation | async-start | bytes 3145728 | tf_op jit(solution)/shard_map/all_to_all | solution.py:28
  56.4 575.5 %all-reduce.58.cloned.1.call-start = ((), (), s32[]{:S(2)}) async-start(), calls=%async_computation.2 | async-start | bytes 442368 | tf_op jit(solution)/shard_map/psum | solution.py:141
  56.4 80.8 %copy-start.10 = (pred[1024]{0:T(1024)(128)(4,1)}, pred[1024]{0:T(1024)(128)(4,1)S(1)}, u32[]{:S(2)}) copy-start(pred[1024]{0:T(1024)(128)(4,1)S(1)} %and_and_fusion.8) | copy-start | bytes 3076
  56.5 80.5 %copy-start.1 = (pred[1024]{0:T(1024)(128)(4,1)}, pred[1024]{0:T(1024)(128)(4,1)S(1)}, u32[]{:S(2)}) copy-start(pred[1024]{0:T(1024)(128)(4,1)S(1)} %get-tuple-element.76) | copy-start | bytes 3076
  56.5 80.5 %copy-start.3 = (pred[1024]{0:T(1024)(128)(4,1)}, pred[1024]{0:T(1024)(128)(4,1)S(1)}, u32[]{:S(2)}) copy-start(pred[1024]{0:T(1024)(128)(4,1)S(1)} %get-tuple-element.77) | copy-start | bytes 3076
  56.6 80.4 %copy-start.5 = (pred[1024]{0:T(1024)(128)(4,1)}, pred[1024]{0:T(1024)(128)(4,1)S(1)}, u32[]{:S(2)}) copy-start(pred[1024]{0:T(1024)(128)(4,1)S(1)} %get-tuple-element.74) | copy-start | bytes 3076
  56.6 80.4 %copy-start.7 = (pred[1024]{0:T(1024)(128)(4,1)}, pred[1024]{0:T(1024)(128)(4,1)S(1)}, u32[]{:S(2)}) copy-start(pred[1024]{0:T(1024)(128)(4,1)S(1)} %get-tuple-element.75) | copy-start | bytes 3076
  122.4 16.6 %collective-permute-start.3 = (bf16[8,1,8,128]{3,0,2,1:T(8,128)(2,1)S(1)}, bf16[8,1,8,128]{3,0,2,1:T(8,128)(2,1)S(1)}, u32[]{:S(2)}, u32[]{:S(2)}) collective-permute-start(bf16[8,1,8,128]{3,0,2,1:T(8,128)(2,1)S(1)} %bitcast.392), channel_id=1, source_target_pairs={{1,0},{2,1},{3,2},{4,3},{5,4},{6,5},{7,6},{8,7},{9,8},{10,9},{11,1... | collective-permute-start | bytes 49160 | tf_op jit(solution)/shard_map/ppermute | solution.py:19
  124.3 14.7 %collective-permute-start.2 = (bf16[8,1,8,128]{3,0,2,1:T(8,128)(2,1)S(1)}, bf16[8,1,8,128]{3,0,2,1:T(8,128)(2,1)S(1)}, u32[]{:S(2)}, u32[]{:S(2)}) collective-permute-start(bf16[8,1,8,128]{3,0,2,1:T(8,128)(2,1)S(1)} %bitcast.393), channel_id=1, source_target_pairs={{0,1},{1,2},{2,3},{3,4},{4,5},{5,6},{6,7},{7,8},{8,9},{9,10},{10,1... | collective-permute-start | bytes 49160 | tf_op jit(solution)/shard_map/ppermute | solution.py:17
  138.9 494.6 %all-gather.2.cloned.1.call-start = ((), (), s32[]{:S(2)}) async-start(), calls=%async_computation.1 | async-start | bytes 5271552 | tf_op jit(solution)/shard_map/all_gather | solution.py:45
  633.5 2.0 slice-start
  639.2 1.4 slice-start.1
  643.4 1.9 copy-start.2
  643.4 1.9 copy-start.4
  643.4 1.9 copy-start.6
  643.4 1.9 copy-start.8
  643.4 1.9 copy-start.11
Sparse Core Ops, SparseCore 0:
  139.0 492.8 all-reduce.57
Sparse Core Ops, SparseCore 1:
  142.1 218.5 all-gather.1
where the time goes:
time: 654 us
  waiting for transfers between devices  438 us (67%)
  blocking collectives  129 us (20%)
  starting transfers between devices  48.3 us (7%)
  between operations  16 us (2%)
  local copies, waits for them, and re-layouts  12.3 us (2%)
    psum x1, waiting for transfers between devices, on_device(): kernel_total, bias_total = lax.psum((kernel_part, bias_part), 'slab')  362 us
    psum x1, blocking collectives, on_device(): kernel_total, bias_total = lax.psum((kernel_part, bias_part), 'slab')  129 us
    all_to_all x1, waiting for transfers between devices, copy_for_each(): return lax.all_to_all(copies, axis, split_axis=0, concat_axis=0, tiled=True)  64 us
    ppermute x2, starting transfers between devices, padded(): lax.ppermute(tail, axis, [(i, (i + 1) % count) for i in range(ends)])  29.2 us
    all_to_all x1, starting transfers between devices, copy_for_each(): return lax.all_to_all(copies, axis, split_axis=0, concat_axis=0, tiled=True)  15.2 us
  transfers between devices with their start and end apart: 7, of which 3 were waited for; matrix products, arithmetic and copies ran while one was open for 1% of the time, Pallas kernels for 0%

commit v1 on v0

v1 whole, which is shorter than its diff:
```python
import math

import jax
import jax.numpy as jnp
from jax import lax
from jax.sharding import PartitionSpec as P


def silu_grad(values):
    sig = jax.nn.sigmoid(values)
    return sig * (1.0 + values * (1.0 - sig))


def shifted_cells(values, high_step, wide_step, n_high, n_wide):
    length = values.shape[-1]
    offset = high_step * n_wide + wide_step
    if offset > 0:
        filler = jnp.zeros(values.shape[:-1] + (offset,), values.dtype)
        moved = jnp.concatenate([values[..., offset:], filler], axis=-1)
    elif offset < 0:
        filler = jnp.zeros(values.shape[:-1] + (-offset,), values.dtype)
        moved = jnp.concatenate([filler, values[..., :offset]], axis=-1)
    else:
        moved = values
    position = lax.iota(jnp.int32, length)
    high_index = position // n_wide % n_high + high_step
    wide_index = position % n_wide + wide_step
    valid = (high_index >= 0) & (high_index < n_high) & (wide_index >= 0) & (wide_index < n_wide)
    return jnp.where(valid, moved, jnp.zeros_like(moved))


def from_below(values, axis):
    count = lax.axis_size(axis)
    return lax.ppermute(values, axis, [(i, i + 1) for i in range(count - 1)])


def from_above(values, axis):
    count = lax.axis_size(axis)
    return lax.ppermute(values, axis, [(i + 1, i) for i in range(count - 1)])


def tap_sums(products, sign, n_high, n_wide):
    sums = []
    for depth_tap in range(3):
        total = None
        for high_tap in range(3):
            for wide_tap in range(3):
                moved = shifted_cells(
                    products[depth_tap, high_tap, wide_tap],
                    sign * (high_tap - 1),
                    sign * (wide_tap - 1),
                    n_high,
                    n_wide,
                )
                total = moved if total is None else total + moved
        sums.append(total)
    return sums


def on_device(inputs, weight, conv_bias, out_grad):
    n_local, n_depth, n_high, n_wide = inputs.shape
    n_chan = weight.shape[4]
    cells = n_depth * n_high * n_wide
    grad_scale = 1.0 / math.sqrt(cells * lax.axis_size("slab"))

    weight_flat = weight.reshape(n_local, 27, n_chan)
    weight_cols = lax.all_to_all(weight_flat, "chan", split_axis=2, concat_axis=0, tiled=True)

    in_flat = inputs.reshape(n_local, cells)
    in_all = lax.all_gather(in_flat, "chan", axis=0, tiled=True)
    weight_rows = weight_flat.transpose(1, 0, 2).reshape(27 * n_local, n_chan)
    products = jnp.dot(weight_rows, in_all, preferred_element_type=jnp.float32)
    products = products.reshape(3, 3, 3, n_local, cells)
    fwd = tap_sums(products, 1, n_high, n_wide)
    pre_sum = fwd[1] + from_below(fwd[0], "slab") + from_above(fwd[2], "slab")
    pre_sum = pre_sum + conv_bias.astype(jnp.float32)[:, None]
    activated = jax.nn.silu(pre_sum).astype(jnp.bfloat16).reshape(inputs.shape)
    slope = (out_grad.reshape(n_local, cells).astype(jnp.float32) * silu_grad(pre_sum)).astype(
        jnp.bfloat16
    )

    slope_below = from_below(slope, "slab")
    slope_above = from_above(slope, "slab")
    slope_planes = (slope_above, slope, slope_below)
    slope_moved = jnp.stack(
        [
            shifted_cells(slope_planes[depth_tap], 1 - high_tap, 1 - wide_tap, n_high, n_wide)
            for depth_tap in range(3)
            for high_tap in range(3)
            for wide_tap in range(3)
        ],
        axis=0,
    ).reshape(27 * n_local, cells)
    tap_grad = lax.dot_general(
        slope_moved, in_all, (((1,), (1,)), ((), ())), preferred_element_type=jnp.float32
    )
    kernel_part = tap_grad.reshape(27, n_local, n_chan).transpose(1, 0, 2)
    bias_part = jnp.sum(slope.astype(jnp.float32), axis=1)
    bias_row = jnp.zeros((n_local, 1, n_chan), jnp.float32).at[:, 0, 0].set(bias_part)
    both = jnp.concatenate([kernel_part, bias_row], axis=1)
    n_slab = lax.axis_size("slab")
    pieces = lax.all_to_all(both.reshape(n_slab, -1), "slab", split_axis=0, concat_axis=0, tiled=True)
    summed = jnp.sum(pieces, axis=0, keepdims=True)
    total = lax.all_gather(summed, "slab", axis=0, tiled=True).reshape(n_local, 28, n_chan)
    kernel_total = total[:, :27].reshape(n_local, 3, 3, 3, n_chan) * grad_scale
    bias_total = total[:, 27, 0] * grad_scale

    slope_all = lax.all_gather(slope, "chan", axis=0, tiled=True)
    back = lax.dot_general(
        weight_cols.reshape(n_chan, 27 * n_local),
        slope_all,
        (((0,), (0,)), ((), ())),
        preferred_element_type=jnp.float32,
    )
    back = back.reshape(3, 3, 3, n_local, cells)
    bwd = tap_sums(back, -1, n_high, n_wide)
    back_total = bwd[1] + from_above(bwd[0], "slab") + from_below(bwd[2], "slab")
    input_grad = back_total.astype(jnp.bfloat16).reshape(inputs.shape)
    return (activated, input_grad, kernel_total, bias_total)


def solution(mesh):
    placed = (
        P("chan", "slab", None, None),
        P("chan", None, None, None, None),
        P("chan"),
        P("chan", "slab", None, None),
    )
    return jax.shard_map(
        on_device,
        mesh=mesh,
        in_specs=placed,
        out_specs=(
            P("chan", "slab", None, None),
            P("chan", "slab", None, None),
            P("chan", None, None, None, None),
            P("chan"),
        ),
        check_vma=False,
    )
```

time: 654 us -> 437 us (0.67)
  waiting for transfers between devices: 438 us -> 27 us
  blocking collectives: 129 us -> 291 us
  starting transfers between devices: 48.3 us -> 96 us
  between operations: 16 us -> 1.15 us
    psum x1 -> x0, waiting for transfers between devices: 362 us -> none  [on_device(): kernel_total, bias_total = lax.psum((kernel_part, bias_part), 'slab')]
    all_gather x0 -> x3, blocking collectives: none -> 291 us  [the longest x1 110 us: on_device(): in_all = lax.all_gather(in_flat, 'chan', axis=0, tiled=True)]
    psum x1 -> x0, blocking collectives: 129 us -> none  [on_device(): kernel_total, bias_total = lax.psum((kernel_part, bias_part), 'slab')]
    all_to_all x1 -> x2, waiting for transfers between devices: 64 us -> 0.01 us  [the longest x1 0.01 us: on_device(): lax.all_to_all(both.reshape(n_slab, -1), 'slab', split_axis=0, concat_axi...]
    ppermute x4 -> x6, starting transfers between devices: 33 us -> 65.7 us  [the longest x3 45.7 us: from_below(): return lax.ppermute(values, axis, [(i, i + 1) for i in range(count - 1)])]
    all_to_all x1 -> x2, starting transfers between devices: 15.2 us -> 30.3 us  [the longest x1 15.9 us: on_device(): lax.all_to_all(weight_flat, 'chan', split_axis=2, concat_axis=0, tiled=True)]
    ppermute x4 -> x6, waiting for transfers between devices: 12.1 us -> 27 us  [the longest x3 26.3 us: from_above(): return lax.ppermute(values, axis, [(i + 1, i) for i in range(count - 1)])]
    slice x7 -> x0, local copies, waits for them, and re-layouts: 7.72 us -> none  [the longest x6 7.71 us: sent_together(): slab = whole[..., at:at + column.shape[along]]]
  transfers between devices with their start and end apart: 7 -> 8, of which waited for: 3 -> 3; matrix products, arithmetic and copies ran while one was open for 1% -> 3% of each run, Pallas kernels for 0% -> 0%
where the time goes in v1:
time: 437 us
  blocking collectives  291 us (67%)
  starting transfers between devices  96 us (22%)
  waiting for transfers between devices  27 us (6%)
  local copies, waits for them, and re-layouts  16.1 us (4%)
    all_gather x1, blocking collectives, on_device(): in_all = lax.all_gather(in_flat, 'chan', axis=0, tiled=True)  110 us
    all_gather x1, blocking collectives, on_device(): slope_all = lax.all_gather(slope, 'chan', axis=0, tiled=True)  102 us
    all_gather x1, blocking collectives, on_device(): lax.all_gather(summed, 'slab', axis=0, tiled=True)  79.3 us
    ppermute x3, starting transfers between devices, from_below(): return lax.ppermute(values, axis, [(i, i + 1) for i in range(count - 1)])  45.7 us
    ppermute x3, waiting for transfers between devices, from_above(): return lax.ppermute(values, axis, [(i + 1, i) for i in range(count - 1)])  26.3 us
    ppermute x3, starting transfers between devices, from_above(): return lax.ppermute(values, axis, [(i + 1, i) for i in range(count - 1)])  20 us
    all_to_all x1, starting transfers between devices, on_device(): lax.all_to_all(weight_flat, 'chan', split_axis=2, concat_axis=0, tiled=True)  15.9 us
    all_to_all x1, starting transfers between devices, on_device(): lax.all_to_all(both.reshape(n_slab, -1), 'slab', split_axis=0, concat_axi...  14.4 us
  transfers between devices with their start and end apart: 8, of which 3 were waited for; matrix products, arithmetic and copies ran while one was open for 3% of the time, Pallas kernels for 0%

profile of v1, /device:TPU:1, one launch (start us, length us, event | category | flops | bytes accessed | tf_op | source)
XLA Modules:
  0.0 436.6 jit_solution(12345620119673896778)
XLA Ops:
  0.6 1.3 copy.45
  2.0 1.7 reshape.102
  3.7 15.9 %all-to-all-start = ((bf16[32,2,864]{2,1,0:T(2,128)(2,1)}), bf16[32,2,864]{2,1,0:T(2,128)(2,1)S(1)}, u32[]{:S(2)}, u32[]{:S(2)}) async-start(bf16[32,2,864]{2,1,0:T(2,128)(2,1)} %reshape.102), calls=%async_computation | async-start | bytes 229376 | tf_op jit(solution)/shard_map/all_to_all | solution.py:67
  19.7 0.7 copy.63
  20.4 110.3 %all_gather.9 = bf16[256,1024]{1,0:T(8,128)(2,1)S(1)} all-gather(bf16[8,1024]{1,0:T(8,128)(2,1)S(1)} %bitcast.335), channel_id=1, replica_groups=mesh['chan'=32,'slab'=32] {'chan'}, dimensions={0}, use_global_device_ids=true | all-gather | bytes 540672 | tf_op jit(solution)/shard_map/all_gather | solution.py:70
  130.8 0.3 fusion
  131.5 30.6 %collective-permute-start = (f32[8,1024]{1,0:T(8,128)S(1)}, f32[8,1024]{1,0:T(8,128)S(1)}, u32[]{:S(2)}, u32[]{:S(2)}) collective-permute-start(f32[8,1024]{1,0:T(8,128)S(1)} %fusion.37), channel_id=1, source_target_pairs={{0,1},{1,2},{2,3},{3,4},{4,5},{5,6},{6,7},{7,8},{8,9},{9,10},{10,1... | collective-permute-start | bytes 98312 | tf_op jit(solution)/shard_map/ppermute | solution.py:34
  162.5 1.9 collective-permute-start.1
  164.7 13.0 %collective-permute-done.1 = f32[8,1024]{1,0:T(8,128)S(1)} collective-permute-done((f32[8,1024]{1,0:T(8,128)S(1)}, f32[8,1024]{1,0:T(8,128)S(1)}, u32[]{:S(2)}, u32[]{:S(2)}) %collective-permute-start.1) | collective-permute-done | bytes 32800 | tf_op jit(solution)/shard_map/ppermute | solution.py:39
  177.7 0.2 convert_reduce_fusion
  177.9 1.9 collective-permute-start.5
  179.9 2.4 collective-permute-start.4
  182.6 13.3 %collective-permute-done.4 = bf16[8,1024]{1,0:T(8,128)(2,1)S(1)} collective-permute-done((bf16[8,1024]{1,0:T(8,128)(2,1)S(1)}, bf16[8,1024]{1,0:T(8,128)(2,1)S(1)}, u32[]{:S(2)}, u32[]{:S(2)}) %collective-permute-start.4) | collective-permute-done | bytes 16416 | tf_op jit(solution)/shard_map/ppermute | solution.py:39
  197.4 0.3 convolution_bitcast_fusion
  197.8 0.9 all_to_all.22
  198.8 14.4 %all-to-all-start.1 = ((f32[32,1,1792]{2,1,0:T(1,128)}), f32[32,1,1792]{2,1,0:T(1,128)S(1)}, u32[]{:S(2)}, u32[]{:S(2)}) async-start(f32[32,1,1792]{2,1,0:T(1,128)} %all_to_all.22), calls=%async_computation.1 | async-start | bytes 458752 | tf_op jit(solution)/shard_map/all_to_all | solution.py:102
  213.2 0.6 copy.52
  213.8 101.8 %all_gather.10 = bf16[256,1024]{1,0:T(8,128)(2,1)S(1)} all-gather(bf16[8,1024]{1,0:T(8,128)(2,1)S(1)} %get-tuple-element.41), channel_id=1, replica_groups=mesh['chan'=32,'slab'=32] {'chan'}, dimensions={0}, use_global_device_ids=true | all-gather | bytes 540672 | tf_op jit(solution)/shard_map/all_gather | solution.py:108
  315.6 1.4 reshape.103
  317.0 3.4 copy.47
  320.4 2.9 reshape.87
  323.3 0.3 fusion.80
  324.2 0.1 fusion.16
  324.3 15.7 %collective-permute-start.2 = (f32[8,1024]{1,0:T(8,128)S(1)}, f32[8,1024]{1,0:T(8,128)S(1)}, u32[]{:S(2)}, u32[]{:S(2)}) collective-permute-start(f32[8,1024]{1,0:T(8,128)S(1)} %fusion.16), channel_id=1, source_target_pairs={{1,0},{2,1},{3,2},{4,3},{5,4},{6,5},{7,6},{8,7},{9,8},{10,9},{11,1... | collective-permute-start | bytes 98312 | tf_op jit(solution)/shard_map/ppermute | solution.py:39
  340.1 13.2 %collective-permute-start.3 = (f32[8,1024]{1,0:T(8,128)S(1)}, f32[8,1024]{1,0:T(8,128)S(1)}, u32[]{:S(2)}, u32[]{:S(2)}) collective-permute-start(f32[8,1024]{1,0:T(8,128)S(1)} %fusion.10), channel_id=1, source_target_pairs={{0,1},{1,2},{2,3},{3,4},{4,5},{5,6},{6,7},{7,8},{8,9},{9,10},{10,1... | collective-permute-start | bytes 98312 | tf_op jit(solution)/shard_map/ppermute | solution.py:34
  353.6 0.7 collective-permute-done.3
  354.4 0.6 copy.53
  355.0 0.1 reduce_sum.19
  355.2 79.3 %all-gather.1 = f32[32,1,1792]{2,1,0:T(1,128)S(1)} all-gather(f32[1,1,1792]{2,1,0:T(1,128)S(1)} %reshape.95), channel_id=2, replica_groups=mesh['chan'=32,'slab'=32] {'slab'}, dimensions={0}, use_global_device_ids=true | all-gather | bytes 236544 | tf_op jit(solution)/shard_map/all_gather | solution.py:104
  434.5 0.5 reduce.3
  435.1 0.7 fusion.65
  435.7 0.8 copy_multiply_fusion
  (107 shorter events, 3.9 us)
Async XLA Ops:
  0.6 130.1 %copy-start = (bf16[8,3,3,3,256]{4,0,3,2,1:T(8,128)(2,1)S(1)}, bf16[8,3,3,3,256]{4,0,3,2,1:T(8,128)(2,1)}, u32[]{:S(2)}) copy-start(bf16[8,3,3,3,256]{4,0,3,2,1:T(8,128)(2,1)} %param.7) | copy-start | bytes 331780
  3.7 195.1 %all-to-all-start = ((bf16[32,2,864]{2,1,0:T(2,128)(2,1)}), bf16[32,2,864]{2,1,0:T(2,128)(2,1)S(1)}, u32[]{:S(2)}, u32[]{:S(2)}) async-start(bf16[32,2,864]{2,1,0:T(2,128)(2,1)} %reshape.102), calls=%async_computation | async-start | bytes 229376 | tf_op jit(solution)/shard_map/all_to_all | solution.py:67
  131.1 33.4 %copy-start.1 = (bf16[8,1,8,128]{3,2,1,0:T(8,128)(2,1)S(1)}, bf16[8,1,8,128]{3,2,1,0:T(8,128)(2,1)}, u32[]{:S(2)}) copy-start(bf16[8,1,8,128]{3,2,1,0:T(8,128)(2,1)} %param.9) | copy-start | bytes 49156
  131.1 33.4 %copy-start.2 = (bf16[8]{0:T(256)(128)(2,1)S(1)}, bf16[8]{0:T(256)(128)(2,1)}, u32[]{:S(2)}) copy-start(bf16[8]{0:T(256)(128)(2,1)} %param.8) | copy-start | bytes 52
  131.5 33.2 %collective-permute-start = (f32[8,1024]{1,0:T(8,128)S(1)}, f32[8,1024]{1,0:T(8,128)S(1)}, u32[]{:S(2)}, u32[]{:S(2)}) collective-permute-start(f32[8,1024]{1,0:T(8,128)S(1)} %fusion.37), channel_id=1, source_target_pairs={{0,1},{1,2},{2,3},{3,4},{4,5},{5,6},{6,7},{7,8},{8,9},{9,10},{10,1... | collective-permute-start | bytes 98312 | tf_op jit(solution)/shard_map/ppermute | solution.py:34
  162.5 15.2 %collective-permute-start.1 = (f32[8,1024]{1,0:T(8,128)S(1)}, f32[8,1024]{1,0:T(8,128)S(1)}, u32[]{:S(2)}, u32[]{:S(2)}) collective-permute-start(f32[8,1024]{1,0:T(8,128)S(1)} %fusion.31), channel_id=1, source_target_pairs={{1,0},{2,1},{3,2},{4,3},{5,4},{6,5},{7,6},{8,7},{9,8},{10,9},{11,1... | collective-permute-start | bytes 98312 | tf_op jit(solution)/shard_map/ppermute | solution.py:39
  177.9 18.9 %collective-permute-start.5 = (bf16[8,1024]{1,0:T(8,128)(2,1)S(1)}, bf16[8,1024]{1,0:T(8,128)(2,1)S(1)}, u32[]{:S(2)}, u32[]{:S(2)}) collective-permute-start(bf16[8,1024]{1,0:T(8,128)(2,1)S(1)} %get-tuple-element.41), channel_id=1, source_target_pairs={{0,1},{1,2},{2,3},{3,4},{4,5},{5,6},{6,7},{7,8},{8,9},{9,10},{10,1... | collective-permute-start | bytes 49160 | tf_op jit(solution)/shard_map/ppermute | solution.py:34
  179.9 16.0 %collective-permute-start.4 = (bf16[8,1024]{1,0:T(8,128)(2,1)S(1)}, bf16[8,1024]{1,0:T(8,128)(2,1)S(1)}, u32[]{:S(2)}, u32[]{:S(2)}) collective-permute-start(bf16[8,1024]{1,0:T(8,128)(2,1)S(1)} %get-tuple-element.41), channel_id=1, source_target_pairs={{1,0},{2,1},{3,2},{4,3},{5,4},{6,5},{7,6},{8,7},{9,8},{10,9},{11,1... | collective-permute-start | bytes 49160 | tf_op jit(solution)/shard_map/ppermute | solution.py:39
  198.8 156.3 %all-to-all-start.1 = ((f32[32,1,1792]{2,1,0:T(1,128)}), f32[32,1,1792]{2,1,0:T(1,128)S(1)}, u32[]{:S(2)}, u32[]{:S(2)}) async-start(f32[32,1,1792]{2,1,0:T(1,128)} %all_to_all.22), calls=%async_computation.1 | async-start | bytes 458752 | tf_op jit(solution)/shard_map/all_to_all | solution.py:102
  324.3 29.3 %collective-permute-start.2 = (f32[8,1024]{1,0:T(8,128)S(1)}, f32[8,1024]{1,0:T(8,128)S(1)}, u32[]{:S(2)}, u32[]{:S(2)}) collective-permute-start(f32[8,1024]{1,0:T(8,128)S(1)} %fusion.16), channel_id=1, source_target_pairs={{1,0},{2,1},{3,2},{4,3},{5,4},{6,5},{7,6},{8,7},{9,8},{10,9},{11,1... | collective-permute-start | bytes 98312 | tf_op jit(solution)/shard_map/ppermute | solution.py:39
  340.1 14.2 %collective-permute-start.3 = (f32[8,1024]{1,0:T(8,128)S(1)}, f32[8,1024]{1,0:T(8,128)S(1)}, u32[]{:S(2)}, u32[]{:S(2)}) collective-permute-start(f32[8,1024]{1,0:T(8,128)S(1)} %fusion.10), channel_id=1, source_target_pairs={{0,1},{1,2},{2,3},{3,4},{4,5},{5,6},{6,7},{7,8},{8,9},{9,10},{10,1... | collective-permute-start | bytes 98312 | tf_op jit(solution)/shard_map/ppermute | solution.py:34

commit v2 on v1

--- a/solution.py
+++ b/solution.py
@@ -39,6 +39,13 @@
     return lax.ppermute(values, axis, [(i + 1, i) for i in range(count - 1)])
 
 
+def gathered(values, axis):
+    count = lax.axis_size(axis)
+    copies = jnp.broadcast_to(values[None], (count, *values.shape))
+    blocks = lax.all_to_all(copies, axis, split_axis=0, concat_axis=0, tiled=True)
+    return blocks.reshape(count * values.shape[0], *values.shape[1:])
+
+
 def tap_sums(products, sign, n_high, n_wide):
     sums = []
     for depth_tap in range(3):
@@ -67,7 +74,7 @@
     weight_cols = lax.all_to_all(weight_flat, "chan", split_axis=2, concat_axis=0, tiled=True)
 
     in_flat = inputs.reshape(n_local, cells)
-    in_all = lax.all_gather(in_flat, "chan", axis=0, tiled=True)
+    in_all = gathered(in_flat, "chan")
     weight_rows = weight_flat.transpose(1, 0, 2).reshape(27 * n_local, n_chan)
     products = jnp.dot(weight_rows, in_all, preferred_element_type=jnp.float32)
     products = products.reshape(3, 3, 3, n_local, cells)
@@ -101,11 +108,11 @@
     n_slab = lax.axis_size("slab")
     pieces = lax.all_to_all(both.reshape(n_slab, -1), "slab", split_axis=0, concat_axis=0, tiled=True)
     summed = jnp.sum(pieces, axis=0, keepdims=True)
-    total = lax.all_gather(summed, "slab", axis=0, tiled=True).reshape(n_local, 28, n_chan)
+    total = gathered(summed, "slab").reshape(n_local, 28, n_chan)
     kernel_total = total[:, :27].reshape(n_local, 3, 3, 3, n_chan) * grad_scale
     bias_total = total[:, 27, 0] * grad_scale
 
-    slope_all = lax.all_gather(slope, "chan", axis=0, tiled=True)
+    slope_all = gathered(slope, "chan")
     back = lax.dot_general(
         weight_cols.reshape(n_chan, 27 * n_local),
         slope_all,

time: 437 us -> 271 us (0.62)
  the two profiles are of different devices: /device:TPU:1 before, /device:TPU:33 now
where the time goes in v2:
time: 271 us; the launch traced here: 270 us
  waiting for transfers between devices  107 us (39%)
  starting transfers between devices  90.4 us (33%)
  blocking collectives  47.7 us (18%)
  local copies, waits for them, and re-layouts  17 us (6%)
  other arithmetic  5.33 us (2%)
    all_to_all x1, blocking collectives, gathered(): lax.all_to_all(copies, axis, split_axis=0, concat_axis=0, tiled=True)  47.7 us
    all_to_all x2, waiting for transfers between devices, gathered(): lax.all_to_all(copies, axis, split_axis=0, concat_axis=0, tiled=True)  42.4 us
    all_to_all x1, waiting for transfers between devices, on_device(): lax.all_to_all(both.reshape(n_slab, -1), 'slab', split_axis=0, concat_axi...  38.9 us
    ppermute x3, starting transfers between devices, from_below(): return lax.ppermute(values, axis, [(i, i + 1) for i in range(count - 1)])  32.4 us
    all_to_all x1, starting transfers between devices, on_device(): lax.all_to_all(both.reshape(n_slab, -1), 'slab', split_axis=0, concat_axi...  22.9 us
    all_to_all x2, starting transfers between devices, gathered(): lax.all_to_all(copies, axis, split_axis=0, concat_axis=0, tiled=True)  19.2 us
    ppermute x3, waiting for transfers between devices, from_above(): return lax.ppermute(values, axis, [(i + 1, i) for i in range(count - 1)])  14.7 us
    all_to_all x1, waiting for transfers between devices, on_device(): lax.all_to_all(weight_flat, 'chan', split_axis=2, concat_axis=0, tiled=True)  10.8 us
  transfers between devices with their start and end apart: 10, of which 6 were waited for; matrix products, arithmetic and copies ran while one was open for 6% of the time, Pallas kernels for 0%

profile of v2, /device:TPU:33, one launch (start us, length us, event | category | flops | bytes accessed | tf_op | source)
XLA Modules:
  0.0 270.2 jit_solution(2682858885878015325)
XLA Ops:
  0.6 0.7 copy.63
  1.4 0.9 broadcast_in_dim.267
  2.2 14.7 %all-to-all-start = ((bf16[32,8,1024]{2,1,0:T(8,128)(2,1)}), bf16[32,8,1024]{2,1,0:T(8,128)(2,1)S(1)}, u32[]{:S(2)}, u32[]{:S(2)}) async-start(bf16[32,8,1024]{2,1,0:T(8,128)(2,1)} %broadcast_in_dim.267), calls=%async_computation | async-start | bytes 1048576 | tf_op jit(solution)/shard_map/all_to_all | solution.py:45
  16.9 0.7 convert_element_type.21
  17.7 0.7 convert_bitcast_fusion
  18.4 25.6 %all-to-all-done = bf16[32,8,1024]{2,1,0:T(8,128)(2,1)S(1)} async-done(((bf16[32,8,1024]{2,1,0:T(8,128)(2,1)}), bf16[32,8,1024]{2,1,0:T(8,128)(2,1)S(1)}, u32[]{:S(2)}, u32[]{:S(2)}) %all-to-all-start) | async-done | bytes 524320 | tf_op jit(solution)/shard_map/all_to_all | solution.py:45
  44.0 1.2 fusion.1
  45.6 4.8 %collective-permute-start.1 = (f32[8,1024]{1,0:T(8,128)S(1)}, f32[8,1024]{1,0:T(8,128)S(1)}, u32[]{:S(2)}, u32[]{:S(2)}) collective-permute-start(f32[8,1024]{1,0:T(8,128)S(1)} %fusion.33), channel_id=1, source_target_pairs={{1,0},{2,1},{3,2},{4,3},{5,4},{6,5},{7,6},{8,7},{9,8},{10,9},{11,1... | collective-permute-start | bytes 98312 | tf_op jit(solution)/shard_map/ppermute | solution.py:39
  50.7 15.3 %collective-permute-start = (f32[8,1024]{1,0:T(8,128)S(1)}, f32[8,1024]{1,0:T(8,128)S(1)}, u32[]{:S(2)}, u32[]{:S(2)}) collective-permute-start(f32[8,1024]{1,0:T(8,128)S(1)} %fusion.39), channel_id=1, source_target_pairs={{0,1},{1,2},{2,3},{3,4},{4,5},{5,6},{6,7},{7,8},{8,9},{9,10},{10,1... | collective-permute-start | bytes 98312 | tf_op jit(solution)/shard_map/ppermute | solution.py:34
  66.3 0.8 collective-permute-done.1
  67.4 1.9 collective-permute-start.4
  69.6 12.8 %collective-permute-start.5 = (bf16[8,1024]{1,0:T(8,128)(2,1)S(1)}, bf16[8,1024]{1,0:T(8,128)(2,1)S(1)}, u32[]{:S(2)}, u32[]{:S(2)}) collective-permute-start(bf16[8,1024]{1,0:T(8,128)(2,1)S(1)} %get-tuple-element.41), channel_id=1, source_target_pairs={{0,1},{1,2},{2,3},{3,4},{4,5},{5,6},{6,7},{7,8},{8,9},{9,10},{10,1... | collective-permute-start | bytes 49160 | tf_op jit(solution)/shard_map/ppermute | solution.py:34
  84.5 0.9 all_to_all.34
  85.4 22.9 %all-to-all-start.3 = ((f32[32,1,1792]{2,1,0:T(1,128)}), f32[32,1,1792]{2,1,0:T(1,128)S(1)}, u32[]{:S(2)}, u32[]{:S(2)}) async-start(f32[32,1,1792]{2,1,0:T(1,128)} %all_to_all.34), calls=%async_computation.3 | async-start | bytes 458752 | tf_op jit(solution)/shard_map/all_to_all | solution.py:109
  108.7 1.7 reshape.102
  110.4 38.9 %all-to-all-done.3 = f32[32,1,1792]{2,1,0:T(1,128)S(1)} async-done(((f32[32,1,1792]{2,1,0:T(1,128)}), f32[32,1,1792]{2,1,0:T(1,128)S(1)}, u32[]{:S(2)}, u32[]{:S(2)}) %all-to-all-start.3) | async-done | bytes 229408 | tf_op jit(solution)/shard_map/all_to_all | solution.py:109
  149.4 7.3 %all-to-all-start.2 = ((bf16[32,2,864]{2,1,0:T(2,128)(2,1)}), bf16[32,2,864]{2,1,0:T(2,128)(2,1)S(1)}, u32[]{:S(2)}, u32[]{:S(2)}) async-start(bf16[32,2,864]{2,1,0:T(2,128)(2,1)} %reshape.102), calls=%async_computation.2 | async-start | bytes 229376 | tf_op jit(solution)/shard_map/all_to_all | solution.py:74
  156.8 10.8 %all-to-all-done.2 = bf16[32,2,864]{2,1,0:T(2,128)(2,1)S(1)} async-done(((bf16[32,2,864]{2,1,0:T(2,128)(2,1)}), bf16[32,2,864]{2,1,0:T(2,128)(2,1)S(1)}, u32[]{:S(2)}, u32[]{:S(2)}) %all-to-all-start.2) | async-done | bytes 110624 | tf_op jit(solution)/shard_map/all_to_all | solution.py:74
  167.7 47.7 %all_to_all.40 = f32[32,1,1792]{2,1,0:T(1,128)S(1)} all-to-all(f32[32,1,1792]{2,1,0:T(1,128)S(1)} %broadcast_in_dim.277), channel_id=1, replica_groups=mesh['chan'=32,'slab'=32] {'slab'}, dimensions={0} | all-to-all | bytes 458752 | tf_op jit(solution)/shard_map/all_to_all | solution.py:45
  215.5 0.9 broadcast_in_dim.276
  216.4 4.5 %all-to-all-start.1 = ((bf16[32,8,1024]{2,1,0:T(8,128)(2,1)}), bf16[32,8,1024]{2,1,0:T(8,128)(2,1)S(1)}, u32[]{:S(2)}, u32[]{:S(2)}) async-start(bf16[32,8,1024]{2,1,0:T(8,128)(2,1)} %broadcast_in_dim.276), calls=%async_computation.1 | async-start | bytes 1048576 | tf_op jit(solution)/shard_map/all_to_all | solution.py:45
  220.9 1.4 reshape.103
  222.3 3.4 %copy.47 = bf16[32,8,27,8]{1,0,3,2:T(8,128)(2,1)S(1)} copy(bf16[32,8,27,8]{2,1,3,0:T(8,128)(2,1)S(1)} %bitcast.324) | data formatting | bytes 221184 | tf_op jit(solution)/shard_map/all_to_all | solution.py:74
  225.7 2.9 %reshape.93 = bf16[256,216]{0,1:T(8,128)(2,1)S(1)} reshape(bf16[32,8,27,8]{1,0,3,2:T(8,128)(2,1)S(1)} %copy.47) | data formatting | bytes 221184 | tf_op jit(solution)/shard_map/reshape | solution.py:117
  228.6 0.6 copy.52
  229.8 0.7 fusion.67
  230.5 0.8 copy_multiply_fusion
  231.3 16.8 %all-to-all-done.1 = bf16[32,8,1024]{2,1,0:T(8,128)(2,1)S(1)} async-done(((bf16[32,8,1024]{2,1,0:T(8,128)(2,1)}), bf16[32,8,1024]{2,1,0:T(8,128)(2,1)S(1)}, u32[]{:S(2)}, u32[]{:S(2)}) %all-to-all-start.1) | async-done | bytes 524320 | tf_op jit(solution)/shard_map/all_to_all | solution.py:45
  248.8 4.2 %collective-permute-start.3 = (f32[8,1024]{1,0:T(8,128)S(1)}, f32[8,1024]{1,0:T(8,128)S(1)}, u32[]{:S(2)}, u32[]{:S(2)}) collective-permute-start(f32[8,1024]{1,0:T(8,128)S(1)} %fusion.12), channel_id=1, source_target_pairs={{0,1},{1,2},{2,3},{3,4},{4,5},{5,6},{6,7},{7,8},{8,9},{9,10},{10,1... | collective-permute-start | bytes 98312 | tf_op jit(solution)/shard_map/ppermute | solution.py:34
  253.4 1.9 collective-permute-start.2
  255.6 13.8 %collective-permute-done.2 = f32[8,1024]{1,0:T(8,128)S(1)} collective-permute-done((f32[8,1024]{1,0:T(8,128)S(1)}, f32[8,1024]{1,0:T(8,128)S(1)}, u32[]{:S(2)}, u32[]{:S(2)}) %collective-permute-start.2) | collective-permute-done | bytes 32800 | tf_op jit(solution)/shard_map/ppermute | solution.py:39
  269.6 0.6 copy.53
  (107 shorter events, 6.0 us)
Async XLA Ops:
  2.2 41.7 %all-to-all-start = ((bf16[32,8,1024]{2,1,0:T(8,128)(2,1)}), bf16[32,8,1024]{2,1,0:T(8,128)(2,1)S(1)}, u32[]{:S(2)}, u32[]{:S(2)}) async-start(bf16[32,8,1024]{2,1,0:T(8,128)(2,1)} %broadcast_in_dim.267), calls=%async_computation | async-start | bytes 1048576 | tf_op jit(solution)/shard_map/all_to_all | solution.py:45
  45.6 21.6 %collective-permute-start.1 = (f32[8,1024]{1,0:T(8,128)S(1)}, f32[8,1024]{1,0:T(8,128)S(1)}, u32[]{:S(2)}, u32[]{:S(2)}) collective-permute-start(f32[8,1024]{1,0:T(8,128)S(1)} %fusion.33), channel_id=1, source_target_pairs={{1,0},{2,1},{3,2},{4,3},{5,4},{6,5},{7,6},{8,7},{9,8},{10,9},{11,1... | collective-permute-start | bytes 98312 | tf_op jit(solution)/shard_map/ppermute | solution.py:39
  50.7 16.5 %collective-permute-start = (f32[8,1024]{1,0:T(8,128)S(1)}, f32[8,1024]{1,0:T(8,128)S(1)}, u32[]{:S(2)}, u32[]{:S(2)}) collective-permute-start(f32[8,1024]{1,0:T(8,128)S(1)} %fusion.39), channel_id=1, source_target_pairs={{0,1},{1,2},{2,3},{3,4},{4,5},{5,6},{6,7},{7,8},{8,9},{9,10},{10,1... | collective-permute-start | bytes 98312 | tf_op jit(solution)/shard_map/ppermute | solution.py:34
  67.4 15.1 %collective-permute-start.4 = (bf16[8,1024]{1,0:T(8,128)(2,1)S(1)}, bf16[8,1024]{1,0:T(8,128)(2,1)S(1)}, u32[]{:S(2)}, u32[]{:S(2)}) collective-permute-start(bf16[8,1024]{1,0:T(8,128)(2,1)S(1)} %get-tuple-element.41), channel_id=1, source_target_pairs={{1,0},{2,1},{3,2},{4,3},{5,4},{6,5},{7,6},{8,7},{9,8},{10,9},{11,1... | collective-permute-start | bytes 49160 | tf_op jit(solution)/shard_map/ppermute | solution.py:39
  69.6 13.8 %collective-permute-start.5 = (bf16[8,1024]{1,0:T(8,128)(2,1)S(1)}, bf16[8,1024]{1,0:T(8,128)(2,1)S(1)}, u32[]{:S(2)}, u32[]{:S(2)}) collective-permute-start(bf16[8,1024]{1,0:T(8,128)(2,1)S(1)} %get-tuple-element.41), channel_id=1, source_target_pairs={{0,1},{1,2},{2,3},{3,4},{4,5},{5,6},{6,7},{7,8},{8,9},{9,10},{10,1... | collective-permute-start | bytes 49160 | tf_op jit(solution)/shard_map/ppermute | solution.py:34
  83.5 24.8 %copy-start = (bf16[8,3,3,3,256]{4,0,3,2,1:T(8,128)(2,1)S(1)}, bf16[8,3,3,3,256]{4,0,3,2,1:T(8,128)(2,1)}, u32[]{:S(2)}) copy-start(bf16[8,3,3,3,256]{4,0,3,2,1:T(8,128)(2,1)} %param.7) | copy-start | bytes 331780
  85.4 64.0 %all-to-all-start.3 = ((f32[32,1,1792]{2,1,0:T(1,128)}), f32[32,1,1792]{2,1,0:T(1,128)S(1)}, u32[]{:S(2)}, u32[]{:S(2)}) async-start(f32[32,1,1792]{2,1,0:T(1,128)} %all_to_all.34), calls=%async_computation.3 | async-start | bytes 458752 | tf_op jit(solution)/shard_map/all_to_all | solution.py:109
  149.4 18.3 %all-to-all-start.2 = ((bf16[32,2,864]{2,1,0:T(2,128)(2,1)}), bf16[32,2,864]{2,1,0:T(2,128)(2,1)S(1)}, u32[]{:S(2)}, u32[]{:S(2)}) async-start(bf16[32,2,864]{2,1,0:T(2,128)(2,1)} %reshape.102), calls=%async_computation.2 | async-start | bytes 229376 | tf_op jit(solution)/shard_map/all_to_all | solution.py:74
  216.4 31.8 %all-to-all-start.1 = ((bf16[32,8,1024]{2,1,0:T(8,128)(2,1)}), bf16[32,8,1024]{2,1,0:T(8,128)(2,1)S(1)}, u32[]{:S(2)}, u32[]{:S(2)}) async-start(bf16[32,8,1024]{2,1,0:T(8,128)(2,1)} %broadcast_in_dim.276), calls=%async_computation.1 | async-start | bytes 1048576 | tf_op jit(solution)/shard_map/all_to_all | solution.py:45
  248.8 6.8 %collective-permute-start.3 = (f32[8,1024]{1,0:T(8,128)S(1)}, f32[8,1024]{1,0:T(8,128)S(1)}, u32[]{:S(2)}, u32[]{:S(2)}) collective-permute-start(f32[8,1024]{1,0:T(8,128)S(1)} %fusion.12), channel_id=1, source_target_pairs={{0,1},{1,2},{2,3},{3,4},{4,5},{5,6},{6,7},{7,8},{8,9},{9,10},{10,1... | collective-permute-start | bytes 98312 | tf_op jit(solution)/shard_map/ppermute | solution.py:34
  253.4 16.1 %collective-permute-start.2 = (f32[8,1024]{1,0:T(8,128)S(1)}, f32[8,1024]{1,0:T(8,128)S(1)}, u32[]{:S(2)}, u32[]{:S(2)}) collective-permute-start(f32[8,1024]{1,0:T(8,128)S(1)} %fusion.18), channel_id=1, source_target_pairs={{1,0},{2,1},{3,2},{4,3},{5,4},{6,5},{7,6},{8,7},{9,8},{10,9},{11,1... | collective-permute-start | bytes 98312 | tf_op jit(solution)/shard_map/ppermute | solution.py:39

commit v3 on v2

--- a/solution.py
+++ b/solution.py
@@ -46,6 +46,36 @@
     return blocks.reshape(count * values.shape[0], *values.shape[1:])
 
 
+REDUCE = "pair"
+
+
+def slab_total(both):
+    n_slab = lax.axis_size("slab")
+    if REDUCE == "psum":
+        return lax.psum(both, "slab")
+    if REDUCE == "rs_ag":
+        piece = lax.psum_scatter(both.reshape(n_slab, -1), "slab", scatter_dimension=0, tiled=True)
+        return lax.all_gather(piece, "slab", axis=0, tiled=True).reshape(both.shape)
+    if REDUCE == "rs_a2a":
+        piece = lax.psum_scatter(both.reshape(n_slab, -1), "slab", scatter_dimension=0, tiled=True)
+        return gathered(piece, "slab").reshape(both.shape)
+    if REDUCE == "pair":
+        halves = both.reshape(2, n_slab, -1)
+        parity = lax.axis_index("slab") % 2
+        keep = jnp.where(parity == 0, halves[0], halves[1])
+        give = jnp.where(parity == 0, halves[1], halves[0])
+        sibling = lax.ppermute(give, "slab", [(i, i ^ 1) for i in range(n_slab)])
+        mine = keep + sibling
+        pieces = lax.all_to_all(mine, "slab", split_axis=0, concat_axis=0, tiled=True)
+        pieces = pieces.reshape(n_slab // 2, 2, -1)
+        summed = jnp.sum(pieces, axis=0)
+        blocks = gathered(summed[None], "slab")
+        return blocks.transpose(1, 0, 2).reshape(both.shape)
+    pieces = lax.all_to_all(both.reshape(n_slab, -1), "slab", split_axis=0, concat_axis=0, tiled=True)
+    summed = jnp.sum(pieces, axis=0, keepdims=True)
+    return gathered(summed, "slab").reshape(both.shape)
+
+
 def tap_sums(products, sign, n_high, n_wide):
     sums = []
     for depth_tap in range(3):
@@ -70,11 +100,16 @@
     cells = n_depth * n_high * n_wide
     grad_scale = 1.0 / math.sqrt(cells * lax.axis_size("slab"))
 
+    n_part = lax.axis_size("chan")
     weight_flat = weight.reshape(n_local, 27, n_chan)
-    weight_cols = lax.all_to_all(weight_flat, "chan", split_axis=2, concat_axis=0, tiled=True)
+    weight_split = weight_flat.reshape(n_local, 27, n_part, n_local).transpose(2, 0, 1, 3)
+    in_flat = inputs.reshape(n_local, cells)
+    in_copies = jnp.broadcast_to(in_flat[None], (n_part, n_local, cells))
+    sent = jnp.concatenate([in_copies, weight_split.reshape(n_part, n_local, 27 * n_local)], axis=2)
+    came = lax.all_to_all(sent, "chan", split_axis=0, concat_axis=0, tiled=True)
+    in_all = came[:, :, :cells].reshape(n_chan, cells)
+    weight_cols = came[:, :, cells:].reshape(n_chan, 27, n_local)
 
-    in_flat = inputs.reshape(n_local, cells)
-    in_all = gathered(in_flat, "chan")
     weight_rows = weight_flat.transpose(1, 0, 2).reshape(27 * n_local, n_chan)
     products = jnp.dot(weight_rows, in_all, preferred_element_type=jnp.float32)
     products = products.reshape(3, 3, 3, n_local, cells)
@@ -105,14 +140,12 @@
     bias_part = jnp.sum(slope.astype(jnp.float32), axis=1)
     bias_row = jnp.zeros((n_local, 1, n_chan), jnp.float32).at[:, 0, 0].set(bias_part)
     both = jnp.concatenate([kernel_part, bias_row], axis=1)
-    n_slab = lax.axis_size("slab")
-    pieces = lax.all_to_all(both.reshape(n_slab, -1), "slab", split_axis=0, concat_axis=0, tiled=True)
-    summed = jnp.sum(pieces, axis=0, keepdims=True)
-    total = gathered(summed, "slab").reshape(n_local, 28, n_chan)
+    slope_all = gathered(slope, "chan")
+    both, slope_all = lax.optimization_barrier((both, slope_all))
+    total = slab_total(both)
     kernel_total = total[:, :27].reshape(n_local, 3, 3, 3, n_chan) * grad_scale
     bias_total = total[:, 27, 0] * grad_scale
 
-    slope_all = gathered(slope, "chan")
     back = lax.dot_general(
         weight_cols.reshape(n_chan, 27 * n_local),
         slope_all,

time: 271 us -> 235 us (0.87)
  waiting for transfers between devices: 107 us -> 90.3 us
  starting transfers between devices: 90.4 us -> 74.9 us
  local copies, waits for them, and re-layouts: 17 us -> 9.81 us
  blocking collectives: 47.7 us -> 53 us
    all_to_all x2 -> x1, waiting for transfers between devices: 49.7 us -> 32 us  [on_device(): came = lax.all_to_all(sent, 'chan', split_axis=0, concat_axis=0, tiled=True)]
    all_to_all x2 -> x1, starting transfers between devices: 30.2 us -> 14.7 us  [on_device(): came = lax.all_to_all(sent, 'chan', split_axis=0, concat_axis=0, tiled=True)]
    ppermute x3, starting transfers between devices: 32.4 us -> 43.4 us  [from_below(): return lax.ppermute(values, axis, [(i, i + 1) for i in range(count - 1)])]
    all_to_all x2, starting transfers between devices: 19.2 us -> 8.8 us  [gathered(): lax.all_to_all(copies, axis, split_axis=0, concat_axis=0, tiled=True)]
    ppermute x3, waiting for transfers between devices: 14.7 us -> 24.2 us  [from_above(): return lax.ppermute(values, axis, [(i + 1, i) for i in range(count - 1)])]
    all_to_all x2, waiting for transfers between devices: 42.4 us -> 33 us  [gathered(): lax.all_to_all(copies, axis, split_axis=0, concat_axis=0, tiled=True)]
    all_to_all x1, blocking collectives: 47.7 us -> 53 us  [slab_total(): lax.all_to_all(mine, 'slab', split_axis=0, concat_axis=0, tiled=True)]
    all_to_all x2 -> x1, local copies, waits for them, and re-layouts: 4.32 us -> 0.12 us  [slab_total(): lax.all_to_all(mine, 'slab', split_axis=0, concat_axis=0, tiled=True)]
  transfers between devices with their start and end apart: 10 -> 10, of which waited for: 6 -> 6; matrix products, arithmetic and copies ran while one was open for 6% -> 3% of each run, Pallas kernels for 0% -> 0%
where the time goes in v3:
time: 235 us
  waiting for transfers between devices  90.3 us (38%)
  starting transfers between devices  74.9 us (32%)
  blocking collectives  53 us (23%)
  local copies, waits for them, and re-layouts  9.81 us (4%)
  other arithmetic  4.53 us (2%)
    all_to_all x1, blocking collectives, slab_total(): lax.all_to_all(mine, 'slab', split_axis=0, concat_axis=0, tiled=True)  53 us
    ppermute x3, starting transfers between devices, from_below(): return lax.ppermute(values, axis, [(i, i + 1) for i in range(count - 1)])  43.4 us
    all_to_all x2, waiting for transfers between devices, gathered(): lax.all_to_all(copies, axis, split_axis=0, concat_axis=0, tiled=True)  33 us
    all_to_all x1, waiting for transfers between devices, on_device(): came = lax.all_to_all(sent, 'chan', split_axis=0, concat_axis=0, tiled=True)  32 us
    ppermute x3, waiting for transfers between devices, from_above(): return lax.ppermute(values, axis, [(i + 1, i) for i in range(count - 1)])  24.2 us
    all_to_all x1, starting transfers between devices, on_device(): came = lax.all_to_all(sent, 'chan', split_axis=0, concat_axis=0, tiled=True)  14.7 us
    all_to_all x2, starting transfers between devices, gathered(): lax.all_to_all(copies, axis, split_axis=0, concat_axis=0, tiled=True)  8.8 us
    ppermute x3, starting transfers between devices, from_above(): return lax.ppermute(values, axis, [(i + 1, i) for i in range(count - 1)])  6.09 us
  transfers between devices with their start and end apart: 10, of which 6 were waited for; matrix products, arithmetic and copies ran while one was open for 3% of the time, Pallas kernels for 0%

profile of v3, /device:TPU:33, one launch (start us, length us, event | category | flops | bytes accessed | tf_op | source)
XLA Modules:
  0.0 234.7 jit_solution(4153325326226414077)
XLA Ops:
  0.6 3.0 %reshape_reshape.6 = bf16[8,27,32,8]{3,2,0,1:T(8,128)(2,1)S(1)} reshape(bf16[8,3,3,3,256]{4,0,3,2,1:T(8,128)(2,1)} %param.7) | data formatting | bytes 221184 | tf_op jit(solution)/shard_map/reshape;reshape | solution.py:105
  3.7 0.8 copy.43
  4.5 0.2 copy.44
  4.8 0.9 pad_maximum_fusion
  5.7 14.7 %all-to-all-start = ((bf16[32,8,1240]{2,1,0:T(8,128)(2,1)}), bf16[32,8,1240]{2,1,0:T(8,128)(2,1)S(1)}, u32[]{:S(2)}, u32[]{:S(2)}) async-start(bf16[32,8,1240]{2,1,0:T(8,128)(2,1)} %pad_maximum_fusion), calls=%async_computation | async-start | bytes 1310720 | tf_op jit(solution)/shard_map/all_to_all | solution.py:109
  20.6 32.0 %all-to-all-done = bf16[32,8,1240]{2,1,0:T(8,128)(2,1)S(1)} async-done(((bf16[32,8,1240]{2,1,0:T(8,128)(2,1)}), bf16[32,8,1240]{2,1,0:T(8,128)(2,1)S(1)}, u32[]{:S(2)}, u32[]{:S(2)}) %all-to-all-start) | async-done | bytes 634912 | tf_op jit(solution)/shard_map/all_to_all | solution.py:109
  52.5 0.3 fusion.3
  53.3 19.0 %collective-permute-start = (f32[8,1024]{1,0:T(8,128)S(1)}, f32[8,1024]{1,0:T(8,128)S(1)}, u32[]{:S(2)}, u32[]{:S(2)}) collective-permute-start(f32[8,1024]{1,0:T(8,128)S(1)} %fusion.40), channel_id=1, source_target_pairs={{0,1},{1,2},{2,3},{3,4},{4,5},{5,6},{6,7},{7,8},{8,9},{9,10},{10,1... | collective-permute-start | bytes 98312 | tf_op jit(solution)/shard_map/ppermute | solution.py:34
  72.6 1.9 collective-permute-start.1
  74.8 13.0 %collective-permute-done.1 = f32[8,1024]{1,0:T(8,128)S(1)} collective-permute-done((f32[8,1024]{1,0:T(8,128)S(1)}, f32[8,1024]{1,0:T(8,128)S(1)}, u32[]{:S(2)}, u32[]{:S(2)}) %collective-permute-start.1) | collective-permute-done | bytes 32800 | tf_op jit(solution)/shard_map/ppermute | solution.py:39
  87.8 0.2 convert_reduce_fusion
  88.0 1.9 collective-permute-start.2
  90.2 12.4 %collective-permute-start.3 = (bf16[8,1024]{1,0:T(8,128)(2,1)S(1)}, bf16[8,1024]{1,0:T(8,128)(2,1)S(1)}, u32[]{:S(2)}, u32[]{:S(2)}) collective-permute-start(bf16[8,1024]{1,0:T(8,128)(2,1)S(1)} %get-tuple-element.41), channel_id=1, source_target_pairs={{0,1},{1,2},{2,3},{3,4},{4,5},{5,6},{6,7},{7,8},{8,9},{9,10},{10,1... | collective-permute-start | bytes 49160 | tf_op jit(solution)/shard_map/ppermute | solution.py:34
  102.7 0.9 broadcast_in_dim.276
  103.5 5.0 %all-to-all-start.1 = ((bf16[32,8,1024]{2,1,0:T(8,128)(2,1)}), bf16[32,8,1024]{2,1,0:T(8,128)(2,1)S(1)}, u32[]{:S(2)}, u32[]{:S(2)}) async-start(bf16[32,8,1024]{2,1,0:T(8,128)(2,1)} %broadcast_in_dim.276), calls=%async_computation.1 | async-start | bytes 1048576 | tf_op jit(solution)/shard_map/all_to_all | solution.py:45
  110.0 0.3 convolution_bitcast_fusion
  110.4 18.2 %all-to-all-done.1 = bf16[32,8,1024]{2,1,0:T(8,128)(2,1)S(1)} async-done(((bf16[32,8,1024]{2,1,0:T(8,128)(2,1)}), bf16[32,8,1024]{2,1,0:T(8,128)(2,1)S(1)}, u32[]{:S(2)}, u32[]{:S(2)}) %all-to-all-start.1) | async-done | bytes 524320 | tf_op jit(solution)/shard_map/all_to_all | solution.py:45
  128.7 1.9 collective-permute-start.6
  130.7 1.2 collective-permute-done.6
  132.1 53.0 %all_to_all.24 = f32[32,1,896]{2,1,0:T(1,128)S(1)} all-to-all(f32[32,1,896]{2,1,0:T(1,128)S(1)} %copy.49), channel_id=1, replica_groups=mesh['chan'=32,'slab'=32] {'slab'}, dimensions={0} | all-to-all | bytes 229376 | tf_op jit(solution)/shard_map/all_to_all | solution.py:69
  185.0 0.3 reduce.2
  185.4 0.8 broadcast_in_dim.277
  186.2 3.8 %all-to-all-start.3 = ((f32[32,1,2,896]{3,2,1,0:T(2,128)}), f32[32,1,2,896]{3,2,1,0:T(2,128)S(1)}, u32[]{:S(2)}, u32[]{:S(2)}) async-start(f32[32,1,2,896]{3,2,1,0:T(2,128)} %broadcast_in_dim.277), calls=%async_computation.3 | async-start | bytes 458752 | tf_op jit(solution)/shard_map/all_to_all | solution.py:45
  190.1 0.6 copy.52
  190.8 0.3 fusion
  191.5 2.3 collective-permute-start.4
  194.1 12.0 %collective-permute-start.5 = (f32[8,1024]{1,0:T(8,128)S(1)}, f32[8,1024]{1,0:T(8,128)S(1)}, u32[]{:S(2)}, u32[]{:S(2)}) collective-permute-start(f32[8,1024]{1,0:T(8,128)S(1)} %fusion.13), channel_id=1, source_target_pairs={{0,1},{1,2},{2,3},{3,4},{4,5},{5,6},{6,7},{7,8},{8,9},{9,10},{10,1... | collective-permute-start | bytes 98312 | tf_op jit(solution)/shard_map/ppermute | solution.py:34
  206.4 11.2 %collective-permute-done.4 = f32[8,1024]{1,0:T(8,128)S(1)} collective-permute-done((f32[8,1024]{1,0:T(8,128)S(1)}, f32[8,1024]{1,0:T(8,128)S(1)}, u32[]{:S(2)}, u32[]{:S(2)}) %collective-permute-start.4) | collective-permute-done | bytes 32800 | tf_op jit(solution)/shard_map/ppermute | solution.py:39
  217.7 0.6 copy.53
  218.3 14.8 %all-to-all-done.3 = f32[32,1,2,896]{3,2,1,0:T(2,128)S(1)} async-done(((f32[32,1,2,896]{3,2,1,0:T(2,128)}), f32[32,1,2,896]{3,2,1,0:T(2,128)S(1)}, u32[]{:S(2)}, u32[]{:S(2)}) %all-to-all-start.3) | async-done | bytes 229408 | tf_op jit(solution)/shard_map/all_to_all | solution.py:45
  233.2 0.7 fusion.68
  233.8 0.8 copy_multiply_fusion
  (121 shorter events, 4.6 us)
Async XLA Ops:
  3.7 1.1 copy-start.2
  4.8 15.6 %copy-start.3 = (bf16[8]{0:T(256)(128)(2,1)S(1)}, bf16[8]{0:T(256)(128)(2,1)}, u32[]{:S(2)}) copy-start(bf16[8]{0:T(256)(128)(2,1)} %param.8) | copy-start | bytes 52
  4.8 15.7 %copy-start.1 = (bf16[8,1,8,128]{3,2,1,0:T(8,128)(2,1)S(1)}, bf16[8,1,8,128]{3,2,1,0:T(8,128)(2,1)}, u32[]{:S(2)}) copy-start(bf16[8,1,8,128]{3,2,1,0:T(8,128)(2,1)} %param.9) | copy-start | bytes 49156
  4.8 47.7 %copy-start = (bf16[8,3,3,3,256]{4,0,3,2,1:T(8,128)(2,1)S(1)}, bf16[8,3,3,3,256]{4,0,3,2,1:T(8,128)(2,1)}, u32[]{:S(2)}) copy-start(bf16[8,3,3,3,256]{4,0,3,2,1:T(8,128)(2,1)} %param.7) | copy-start | bytes 331780
  5.7 46.8 %all-to-all-start = ((bf16[32,8,1240]{2,1,0:T(8,128)(2,1)}), bf16[32,8,1240]{2,1,0:T(8,128)(2,1)S(1)}, u32[]{:S(2)}, u32[]{:S(2)}) async-start(bf16[32,8,1240]{2,1,0:T(8,128)(2,1)} %pad_maximum_fusion), calls=%async_computation | async-start | bytes 1310720 | tf_op jit(solution)/shard_map/all_to_all | solution.py:109
  53.3 21.6 %collective-permute-start = (f32[8,1024]{1,0:T(8,128)S(1)}, f32[8,1024]{1,0:T(8,128)S(1)}, u32[]{:S(2)}, u32[]{:S(2)}) collective-permute-start(f32[8,1024]{1,0:T(8,128)S(1)} %fusion.40), channel_id=1, source_target_pairs={{0,1},{1,2},{2,3},{3,4},{4,5},{5,6},{6,7},{7,8},{8,9},{9,10},{10,1... | collective-permute-start | bytes 98312 | tf_op jit(solution)/shard_map/ppermute | solution.py:34
  72.6 15.2 %collective-permute-start.1 = (f32[8,1024]{1,0:T(8,128)S(1)}, f32[8,1024]{1,0:T(8,128)S(1)}, u32[]{:S(2)}, u32[]{:S(2)}) collective-permute-start(f32[8,1024]{1,0:T(8,128)S(1)} %fusion.34), channel_id=1, source_target_pairs={{1,0},{2,1},{3,2},{4,3},{5,4},{6,5},{7,6},{8,7},{9,8},{10,9},{11,1... | collective-permute-start | bytes 98312 | tf_op jit(solution)/shard_map/ppermute | solution.py:39
  88.0 20.5 %collective-permute-start.2 = (bf16[8,1024]{1,0:T(8,128)(2,1)S(1)}, bf16[8,1024]{1,0:T(8,128)(2,1)S(1)}, u32[]{:S(2)}, u32[]{:S(2)}) collective-permute-start(bf16[8,1024]{1,0:T(8,128)(2,1)S(1)} %get-tuple-element.41), channel_id=1, source_target_pairs={{1,0},{2,1},{3,2},{4,3},{5,4},{6,5},{7,6},{8,7},{9,8},{10,9},{11,1... | collective-permute-start | bytes 49160 | tf_op jit(solution)/shard_map/ppermute | solution.py:39
  90.2 19.3 %collective-permute-start.3 = (bf16[8,1024]{1,0:T(8,128)(2,1)S(1)}, bf16[8,1024]{1,0:T(8,128)(2,1)S(1)}, u32[]{:S(2)}, u32[]{:S(2)}) collective-permute-start(bf16[8,1024]{1,0:T(8,128)(2,1)S(1)} %get-tuple-element.41), channel_id=1, source_target_pairs={{0,1},{1,2},{2,3},{3,4},{4,5},{5,6},{6,7},{7,8},{8,9},{9,10},{10,1... | collective-permute-start | bytes 49160 | tf_op jit(solution)/shard_map/ppermute | solution.py:34
  103.5 25.0 %all-to-all-start.1 = ((bf16[32,8,1024]{2,1,0:T(8,128)(2,1)}), bf16[32,8,1024]{2,1,0:T(8,128)(2,1)S(1)}, u32[]{:S(2)}, u32[]{:S(2)}) async-start(bf16[32,8,1024]{2,1,0:T(8,128)(2,1)} %broadcast_in_dim.276), calls=%async_computation.1 | async-start | bytes 1048576 | tf_op jit(solution)/shard_map/all_to_all | solution.py:45
  128.7 3.2 %collective-permute-start.6 = (f32[32,896]{1,0:T(8,128)S(1)}, f32[32,896]{1,0:T(8,128)S(1)}, u32[]{:S(2)}, u32[]{:S(2)}) collective-permute-start(f32[32,896]{1,0:T(8,128)S(1)} %select_n.1254), channel_id=1, source_target_pairs={{0,1},{1,0},{2,3},{3,2},{4,5},{5,4},{6,7},{7,6},{8,9},{9,8},{10,11... | collective-permute-start | bytes 344072 | tf_op jit(solution)/shard_map/ppermute | solution.py:67
  186.2 46.9 %all-to-all-start.3 = ((f32[32,1,2,896]{3,2,1,0:T(2,128)}), f32[32,1,2,896]{3,2,1,0:T(2,128)S(1)}, u32[]{:S(2)}, u32[]{:S(2)}) async-start(f32[32,1,2,896]{3,2,1,0:T(2,128)} %broadcast_in_dim.277), calls=%async_computation.3 | async-start | bytes 458752 | tf_op jit(solution)/shard_map/all_to_all | solution.py:45
  191.5 26.1 %collective-permute-start.4 = (f32[8,1024]{1,0:T(8,128)S(1)}, f32[8,1024]{1,0:T(8,128)S(1)}, u32[]{:S(2)}, u32[]{:S(2)}) collective-permute-start(f32[8,1024]{1,0:T(8,128)S(1)} %fusion.19), channel_id=1, source_target_pairs={{1,0},{2,1},{3,2},{4,3},{5,4},{6,5},{7,6},{8,7},{9,8},{10,9},{11,1... | collective-permute-start | bytes 98312 | tf_op jit(solution)/shard_map/ppermute | solution.py:39
  194.1 23.5 %collective-permute-start.5 = (f32[8,1024]{1,0:T(8,128)S(1)}, f32[8,1024]{1,0:T(8,128)S(1)}, u32[]{:S(2)}, u32[]{:S(2)}) collective-permute-start(f32[8,1024]{1,0:T(8,128)S(1)} %fusion.13), channel_id=1, source_target_pairs={{0,1},{1,2},{2,3},{3,4},{4,5},{5,6},{6,7},{7,8},{8,9},{9,10},{10,1... | collective-permute-start | bytes 98312 | tf_op jit(solution)/shard_map/ppermute | solution.py:34

commit v4 on v3

--- a/solution.py
+++ b/solution.py
@@ -69,8 +69,15 @@
         pieces = lax.all_to_all(mine, "slab", split_axis=0, concat_axis=0, tiled=True)
         pieces = pieces.reshape(n_slab // 2, 2, -1)
         summed = jnp.sum(pieces, axis=0)
-        blocks = gathered(summed[None], "slab")
-        return blocks.transpose(1, 0, 2).reshape(both.shape)
+        sent = summed[jnp.arange(n_slab) % 2]
+        own_half = lax.all_to_all(sent, "slab", split_axis=0, concat_axis=0, tiled=True)
+        other_half = lax.ppermute(own_half, "slab", [(i, i ^ 1) for i in range(n_slab)])
+        full = jnp.where(
+            parity == 0,
+            jnp.stack([own_half, other_half]),
+            jnp.stack([other_half, own_half]),
+        )
+        return full.reshape(both.shape)
     pieces = lax.all_to_all(both.reshape(n_slab, -1), "slab", split_axis=0, concat_axis=0, tiled=True)
     summed = jnp.sum(pieces, axis=0, keepdims=True)
     return gathered(summed, "slab").reshape(both.shape)

time: 235 us -> 228 us (0.970)
  blocking collectives: 53 us -> 0 us
  starting transfers between devices: 74.9 us -> 97.9 us
  waiting for transfers between devices: 90.3 us -> 112 us
    all_to_all x1 -> x0, blocking collectives: 53 us -> none  [slab_total(): lax.all_to_all(mine, 'slab', split_axis=0, concat_axis=0, tiled=True)]
    all_to_all x0 -> x2, waiting for transfers between devices: none -> 47.1 us  [the longest x1 31.4 us: slab_total(): lax.all_to_all(mine, 'slab', split_axis=0, concat_axis=0, tiled=True)]
    all_to_all x0 -> x2, starting transfers between devices: none -> 24.5 us  [the longest x1 20.7 us: slab_total(): lax.all_to_all(mine, 'slab', split_axis=0, concat_axis=0, tiled=True)]
    all_to_all x2 -> x1, waiting for transfers between devices: 33 us -> 18.2 us  [gathered(): lax.all_to_all(copies, axis, split_axis=0, concat_axis=0, tiled=True)]
    ppermute x3, waiting for transfers between devices: 24.2 us -> 13 us  [from_above(): return lax.ppermute(values, axis, [(i + 1, i) for i in range(count - 1)])]
    all_to_all x2 -> x1, starting transfers between devices: 8.8 us -> 5 us  [gathered(): lax.all_to_all(copies, axis, split_axis=0, concat_axis=0, tiled=True)]
  transfers between devices with their start and end apart: 10 -> 12, of which waited for: 6 -> 7; matrix products, arithmetic and copies ran while one was open for 3% -> 3% of each run, Pallas kernels for 0% -> 0%
where the time goes in v4:
time: 228 us; the launch traced here: 227 us
  waiting for transfers between devices  112 us (49%)
  starting transfers between devices  97.9 us (43%)
  local copies, waits for them, and re-layouts  11.1 us (5%)
  other arithmetic  4.57 us (2%)
    ppermute x3, starting transfers between devices, from_below(): return lax.ppermute(values, axis, [(i, i + 1) for i in range(count - 1)])  43.4 us
    all_to_all x1, waiting for transfers between devices, on_device(): came = lax.all_to_all(sent, 'chan', split_axis=0, concat_axis=0, tiled=True)  32 us
    all_to_all x1, waiting for transfers between devices, slab_total(): lax.all_to_all(mine, 'slab', split_axis=0, concat_axis=0, tiled=True)  31.4 us
    all_to_all x1, starting transfers between devices, slab_total(): lax.all_to_all(mine, 'slab', split_axis=0, concat_axis=0, tiled=True)  20.7 us
    all_to_all x1, waiting for transfers between devices, gathered(): lax.all_to_all(copies, axis, split_axis=0, concat_axis=0, tiled=True)  18.2 us
    all_to_all x1, waiting for transfers between devices, slab_total(): lax.all_to_all(sent, 'slab', split_axis=0, concat_axis=0, tiled=True)  15.7 us
    all_to_all x1, starting transfers between devices, on_device(): came = lax.all_to_all(sent, 'chan', split_axis=0, concat_axis=0, tiled=True)  14.7 us
    ppermute x3, waiting for transfers between devices, from_above(): return lax.ppermute(values, axis, [(i + 1, i) for i in range(count - 1)])  13 us
  transfers between devices with their start and end apart: 12, of which 7 were waited for; matrix products, arithmetic and copies ran while one was open for 3% of the time, Pallas kernels for 0%

profile of v4, /device:TPU:33, one launch (start us, length us, event | category | flops | bytes accessed | tf_op | source)
XLA Modules:
  0.0 227.4 jit_solution(2122510742615905663)
XLA Ops:
  0.6 3.0 %reshape_reshape.6 = bf16[8,27,32,8]{3,2,0,1:T(8,128)(2,1)S(1)} reshape(bf16[8,3,3,3,256]{4,0,3,2,1:T(8,128)(2,1)} %param.7) | data formatting | bytes 221184 | tf_op jit(solution)/shard_map/reshape;reshape | solution.py:112
  3.7 0.8 copy.44
  4.8 0.9 pad_maximum_fusion
  5.7 14.7 %all-to-all-start = ((bf16[32,8,1240]{2,1,0:T(8,128)(2,1)}), bf16[32,8,1240]{2,1,0:T(8,128)(2,1)S(1)}, u32[]{:S(2)}, u32[]{:S(2)}) async-start(bf16[32,8,1240]{2,1,0:T(8,128)(2,1)} %pad_maximum_fusion), calls=%async_computation | async-start | bytes 1310720 | tf_op jit(solution)/shard_map/all_to_all | solution.py:116
  20.6 32.0 %all-to-all-done = bf16[32,8,1240]{2,1,0:T(8,128)(2,1)S(1)} async-done(((bf16[32,8,1240]{2,1,0:T(8,128)(2,1)}), bf16[32,8,1240]{2,1,0:T(8,128)(2,1)S(1)}, u32[]{:S(2)}, u32[]{:S(2)}) %all-to-all-start) | async-done | bytes 634912 | tf_op jit(solution)/shard_map/all_to_all | solution.py:116
  52.5 0.3 fusion.3
  53.3 19.0 %collective-permute-start = (f32[8,1024]{1,0:T(8,128)S(1)}, f32[8,1024]{1,0:T(8,128)S(1)}, u32[]{:S(2)}, u32[]{:S(2)}) collective-permute-start(f32[8,1024]{1,0:T(8,128)S(1)} %fusion.40), channel_id=1, source_target_pairs={{0,1},{1,2},{2,3},{3,4},{4,5},{5,6},{6,7},{7,8},{8,9},{9,10},{10,1... | collective-permute-start | bytes 98312 | tf_op jit(solution)/shard_map/ppermute | solution.py:34
  72.6 1.9 collective-permute-start.1
  74.8 13.0 %collective-permute-done.1 = f32[8,1024]{1,0:T(8,128)S(1)} collective-permute-done((f32[8,1024]{1,0:T(8,128)S(1)}, f32[8,1024]{1,0:T(8,128)S(1)}, u32[]{:S(2)}, u32[]{:S(2)}) %collective-permute-start.1) | collective-permute-done | bytes 32800 | tf_op jit(solution)/shard_map/ppermute | solution.py:39
  88.0 1.9 collective-permute-start.2
  90.2 12.4 %collective-permute-start.3 = (bf16[8,1024]{1,0:T(8,128)(2,1)S(1)}, bf16[8,1024]{1,0:T(8,128)(2,1)S(1)}, u32[]{:S(2)}, u32[]{:S(2)}) collective-permute-start(bf16[8,1024]{1,0:T(8,128)(2,1)S(1)} %get-tuple-element.41), channel_id=1, source_target_pairs={{0,1},{1,2},{2,3},{3,4},{4,5},{5,6},{6,7},{7,8},{8,9},{9,10},{10,1... | collective-permute-start | bytes 49160 | tf_op jit(solution)/shard_map/ppermute | solution.py:34
  102.6 0.9 broadcast_in_dim.272
  103.5 5.0 %all-to-all-start.1 = ((bf16[32,8,1024]{2,1,0:T(8,128)(2,1)}), bf16[32,8,1024]{2,1,0:T(8,128)(2,1)S(1)}, u32[]{:S(2)}, u32[]{:S(2)}) async-start(bf16[32,8,1024]{2,1,0:T(8,128)(2,1)} %broadcast_in_dim.272), calls=%async_computation.1 | async-start | bytes 1048576 | tf_op jit(solution)/shard_map/all_to_all | solution.py:45
  110.0 0.3 convolution_bitcast_fusion
  110.4 18.2 %all-to-all-done.1 = bf16[32,8,1024]{2,1,0:T(8,128)(2,1)S(1)} async-done(((bf16[32,8,1024]{2,1,0:T(8,128)(2,1)}), bf16[32,8,1024]{2,1,0:T(8,128)(2,1)S(1)}, u32[]{:S(2)}, u32[]{:S(2)}) %all-to-all-start.1) | async-done | bytes 524320 | tf_op jit(solution)/shard_map/all_to_all | solution.py:45
  128.7 1.9 collective-permute-start.6
  130.7 1.2 collective-permute-done.6
  131.9 0.8 copy.50
  132.7 20.7 %all-to-all-start.2 = ((f32[32,1,896]{2,1,0:T(1,128)}), f32[32,1,896]{2,1,0:T(1,128)S(1)}, u32[]{:S(2)}, u32[]{:S(2)}) async-start(f32[32,1,896]{2,1,0:T(1,128)} %copy.50), calls=%async_computation.2 | async-start | bytes 229376 | tf_op jit(solution)/shard_map/all_to_all | solution.py:69
  153.6 0.6 copy.53
  154.2 0.3 fusion
  154.5 31.4 %all-to-all-done.2 = f32[32,1,896]{2,1,0:T(1,128)S(1)} async-done(((f32[32,1,896]{2,1,0:T(1,128)}), f32[32,1,896]{2,1,0:T(1,128)S(1)}, u32[]{:S(2)}, u32[]{:S(2)}) %all-to-all-start.2) | async-done | bytes 114720 | tf_op jit(solution)/shard_map/all_to_all | solution.py:69
  186.3 0.6 gather_fusion
  186.9 0.8 copy.51
  187.7 3.8 %all-to-all-start.3 = ((f32[32,1,896]{2,1,0:T(1,128)}), f32[32,1,896]{2,1,0:T(1,128)S(1)}, u32[]{:S(2)}, u32[]{:S(2)}) async-start(f32[32,1,896]{2,1,0:T(1,128)} %copy.51), calls=%async_computation.3 | async-start | bytes 229376 | tf_op jit(solution)/shard_map/all_to_all | solution.py:73
  191.9 2.3 collective-permute-start.4
  194.5 12.0 %collective-permute-start.5 = (f32[8,1024]{1,0:T(8,128)S(1)}, f32[8,1024]{1,0:T(8,128)S(1)}, u32[]{:S(2)}, u32[]{:S(2)}) collective-permute-start(f32[8,1024]{1,0:T(8,128)S(1)} %fusion.13), channel_id=1, source_target_pairs={{0,1},{1,2},{2,3},{3,4},{4,5},{5,6},{6,7},{7,8},{8,9},{9,10},{10,1... | collective-permute-start | bytes 98312 | tf_op jit(solution)/shard_map/ppermute | solution.py:34
  206.8 15.7 %all-to-all-done.3 = f32[32,1,896]{2,1,0:T(1,128)S(1)} async-done(((f32[32,1,896]{2,1,0:T(1,128)}), f32[32,1,896]{2,1,0:T(1,128)S(1)}, u32[]{:S(2)}, u32[]{:S(2)}) %all-to-all-start.3) | async-done | bytes 114720 | tf_op jit(solution)/shard_map/all_to_all | solution.py:73
  222.5 2.3 %collective-permute-start.7 = (f32[32,896]{1,0:T(8,128)S(1)}, f32[32,896]{1,0:T(8,128)S(1)}, u32[]{:S(2)}, u32[]{:S(2)}) collective-permute-start(f32[32,896]{1,0:T(8,128)S(1)} %bitcast.339), channel_id=1, source_target_pairs={{0,1},{1,0},{2,3},{3,2},{4,5},{5,4},{6,7},{7,6},{8,9},{9,8},{10,11... | collective-permute-start | bytes 344072 | tf_op jit(solution)/shard_map/ppermute | solution.py:74
  225.0 0.6 copy.54
  225.9 0.7 fusion.68
  226.5 0.8 copy_multiply_fusion
  (128 shorter events, 5.4 us)
Async XLA Ops:
  3.7 1.1 copy-start.2
  4.8 15.6 %copy-start.3 = (bf16[8]{0:T(256)(128)(2,1)S(1)}, bf16[8]{0:T(256)(128)(2,1)}, u32[]{:S(2)}) copy-start(bf16[8]{0:T(256)(128)(2,1)} %param.8) | copy-start | bytes 52
  4.8 15.7 %copy-start.1 = (bf16[8,1,8,128]{3,2,1,0:T(8,128)(2,1)S(1)}, bf16[8,1,8,128]{3,2,1,0:T(8,128)(2,1)}, u32[]{:S(2)}) copy-start(bf16[8,1,8,128]{3,2,1,0:T(8,128)(2,1)} %param.9) | copy-start | bytes 49156
  4.8 47.7 %copy-start = (bf16[8,3,3,3,256]{4,0,3,2,1:T(8,128)(2,1)S(1)}, bf16[8,3,3,3,256]{4,0,3,2,1:T(8,128)(2,1)}, u32[]{:S(2)}) copy-start(bf16[8,3,3,3,256]{4,0,3,2,1:T(8,128)(2,1)} %param.7) | copy-start | bytes 331780
  5.7 46.8 %all-to-all-start = ((bf16[32,8,1240]{2,1,0:T(8,128)(2,1)}), bf16[32,8,1240]{2,1,0:T(8,128)(2,1)S(1)}, u32[]{:S(2)}, u32[]{:S(2)}) async-start(bf16[32,8,1240]{2,1,0:T(8,128)(2,1)} %pad_maximum_fusion), calls=%async_computation | async-start | bytes 1310720 | tf_op jit(solution)/shard_map/all_to_all | solution.py:116
  53.3 21.6 %collective-permute-start = (f32[8,1024]{1,0:T(8,128)S(1)}, f32[8,1024]{1,0:T(8,128)S(1)}, u32[]{:S(2)}, u32[]{:S(2)}) collective-permute-start(f32[8,1024]{1,0:T(8,128)S(1)} %fusion.40), channel_id=1, source_target_pairs={{0,1},{1,2},{2,3},{3,4},{4,5},{5,6},{6,7},{7,8},{8,9},{9,10},{10,1... | collective-permute-start | bytes 98312 | tf_op jit(solution)/shard_map/ppermute | solution.py:34
  72.6 15.2 %collective-permute-start.1 = (f32[8,1024]{1,0:T(8,128)S(1)}, f32[8,1024]{1,0:T(8,128)S(1)}, u32[]{:S(2)}, u32[]{:S(2)}) collective-permute-start(f32[8,1024]{1,0:T(8,128)S(1)} %fusion.34), channel_id=1, source_target_pairs={{1,0},{2,1},{3,2},{4,3},{5,4},{6,5},{7,6},{8,7},{9,8},{10,9},{11,1... | collective-permute-start | bytes 98312 | tf_op jit(solution)/shard_map/ppermute | solution.py:39
  88.0 20.5 %collective-permute-start.2 = (bf16[8,1024]{1,0:T(8,128)(2,1)S(1)}, bf16[8,1024]{1,0:T(8,128)(2,1)S(1)}, u32[]{:S(2)}, u32[]{:S(2)}) collective-permute-start(bf16[8,1024]{1,0:T(8,128)(2,1)S(1)} %get-tuple-element.41), channel_id=1, source_target_pairs={{1,0},{2,1},{3,2},{4,3},{5,4},{6,5},{7,6},{8,7},{9,8},{10,9},{11,1... | collective-permute-start | bytes 49160 | tf_op jit(solution)/shard_map/ppermute | solution.py:39
  90.2 19.3 %collective-permute-start.3 = (bf16[8,1024]{1,0:T(8,128)(2,1)S(1)}, bf16[8,1024]{1,0:T(8,128)(2,1)S(1)}, u32[]{:S(2)}, u32[]{:S(2)}) collective-permute-start(bf16[8,1024]{1,0:T(8,128)(2,1)S(1)} %get-tuple-element.41), channel_id=1, source_target_pairs={{0,1},{1,2},{2,3},{3,4},{4,5},{5,6},{6,7},{7,8},{8,9},{9,10},{10,1... | collective-permute-start | bytes 49160 | tf_op jit(solution)/shard_map/ppermute | solution.py:34
  103.5 25.0 %all-to-all-start.1 = ((bf16[32,8,1024]{2,1,0:T(8,128)(2,1)}), bf16[32,8,1024]{2,1,0:T(8,128)(2,1)S(1)}, u32[]{:S(2)}, u32[]{:S(2)}) async-start(bf16[32,8,1024]{2,1,0:T(8,128)(2,1)} %broadcast_in_dim.272), calls=%async_computation.1 | async-start | bytes 1048576 | tf_op jit(solution)/shard_map/all_to_all | solution.py:45
  128.7 3.2 %collective-permute-start.6 = (f32[32,896]{1,0:T(8,128)S(1)}, f32[32,896]{1,0:T(8,128)S(1)}, u32[]{:S(2)}, u32[]{:S(2)}) collective-permute-start(f32[32,896]{1,0:T(8,128)S(1)} %select_n.1290), channel_id=1, source_target_pairs={{0,1},{1,0},{2,3},{3,2},{4,5},{5,4},{6,7},{7,6},{8,9},{9,8},{10,11... | collective-permute-start | bytes 344072 | tf_op jit(solution)/shard_map/ppermute | solution.py:67
  132.7 53.2 %all-to-all-start.2 = ((f32[32,1,896]{2,1,0:T(1,128)}), f32[32,1,896]{2,1,0:T(1,128)S(1)}, u32[]{:S(2)}, u32[]{:S(2)}) async-start(f32[32,1,896]{2,1,0:T(1,128)} %copy.50), calls=%async_computation.2 | async-start | bytes 229376 | tf_op jit(solution)/shard_map/all_to_all | solution.py:69
  187.7 34.8 %all-to-all-start.3 = ((f32[32,1,896]{2,1,0:T(1,128)}), f32[32,1,896]{2,1,0:T(1,128)S(1)}, u32[]{:S(2)}, u32[]{:S(2)}) async-start(f32[32,1,896]{2,1,0:T(1,128)} %copy.51), calls=%async_computation.3 | async-start | bytes 229376 | tf_op jit(solution)/shard_map/all_to_all | solution.py:73
  191.9 33.0 %collective-permute-start.4 = (f32[8,1024]{1,0:T(8,128)S(1)}, f32[8,1024]{1,0:T(8,128)S(1)}, u32[]{:S(2)}, u32[]{:S(2)}) collective-permute-start(f32[8,1024]{1,0:T(8,128)S(1)} %fusion.19), channel_id=1, source_target_pairs={{1,0},{2,1},{3,2},{4,3},{5,4},{6,5},{7,6},{8,7},{9,8},{10,9},{11,1... | collective-permute-start | bytes 98312 | tf_op jit(solution)/shard_map/ppermute | solution.py:39
  194.5 30.3 %collective-permute-start.5 = (f32[8,1024]{1,0:T(8,128)S(1)}, f32[8,1024]{1,0:T(8,128)S(1)}, u32[]{:S(2)}, u32[]{:S(2)}) collective-permute-start(f32[8,1024]{1,0:T(8,128)S(1)} %fusion.13), channel_id=1, source_target_pairs={{0,1},{1,2},{2,3},{3,4},{4,5},{5,6},{6,7},{7,8},{8,9},{9,10},{10,1... | collective-permute-start | bytes 98312 | tf_op jit(solution)/shard_map/ppermute | solution.py:34
  222.5 3.3 %collective-permute-start.7 = (f32[32,896]{1,0:T(8,128)S(1)}, f32[32,896]{1,0:T(8,128)S(1)}, u32[]{:S(2)}, u32[]{:S(2)}) collective-permute-start(f32[32,896]{1,0:T(8,128)S(1)} %bitcast.339), channel_id=1, source_target_pairs={{0,1},{1,0},{2,3},{3,2},{4,5},{5,4},{6,7},{7,6},{8,9},{9,8},{10,11... | collective-permute-start | bytes 344072 | tf_op jit(solution)/shard_map/ppermute | solution.py:74
